TPU v7x, 32 devices: a whole 2x2x4 slice. The times are simulated.
32 devices in a mesh: groups: 2 (over y), seq: 4 (over z), head: 2 (over x), rep: 2 (over core).
Axes of the slice: x: 2, y: 2, z: 4, core: 2. Of those that a mesh axis runs over, the one named last changes fastest.
Arguments:
- segment_ids: int32 [2048], P(('groups', 'seq')), parts along dimension 0, may hold values from 0 to 3, never falling along the last dimension, each value on 1 to 640 neighbouring positions
- window_query: bfloat16 [2048, 8, 512], P(('groups', 'seq'), 'head', 'rep'), parts along dimension 0, may hold values from -120 to 120
- window_keys: bfloat16 [2048, 512], P(('groups', 'seq'), 'head'), parts along dimension 0, may hold values from -4 to 4
- window_values: bfloat16 [2048, 512], P(('groups', 'seq'), 'head'), parts along dimension 0, may hold values from -6 to 6
- window_grad_out: bfloat16 [2048, 8, 512], P(('groups', 'seq'), 'head', 'rep'), parts along dimension 0, may hold values from -6 to 6
- window_sinks: float32 [8, 8], P('head', 'rep'), may hold values from 1 to 6
- full_query: bfloat16 [2048, 8, 512], P(('groups', 'seq'), 'head', 'rep'), parts along dimension 0, may hold values from -120 to 120
- full_keys: bfloat16 [2048, 512], P(('groups', 'seq'), 'head'), parts along dimension 0, may hold values from -4 to 4
- full_values: bfloat16 [2048, 512], P(('groups', 'seq'), 'head'), parts along dimension 0, may hold values from -6 to 6
- full_grad_out: bfloat16 [2048, 8, 512], P(('groups', 'seq'), 'head', 'rep'), parts along dimension 0, may hold values from -6 to 6
- full_sinks: float32 [8, 8], P('head', 'rep'), may hold values from 1 to 6
Outputs:
- window_dq: bfloat16 [2048, 8, 512], P(('groups', 'seq'), 'head', 'rep'), parts along dimension 0
- window_dk: bfloat16 [2048, 512], P(('groups', 'seq'), 'head'), parts along dimension 0
- window_dv: bfloat16 [2048, 512], P(('groups', 'seq'), 'head'), parts along dimension 0
- full_dq: bfloat16 [2048, 8, 512], P(('groups', 'seq'), 'head', 'rep'), parts along dimension 0
- full_dk: bfloat16 [2048, 512], P(('groups', 'seq'), 'head'), parts along dimension 0
- full_dv: bfloat16 [2048, 512], P(('groups', 'seq'), 'head'), parts along dimension 0
There are 2 independent parts, one for each index of `groups`. A program takes and returns all parts, laid end to end along the dimension named above; an argument that names none is the same for every part. Nothing has to cross between parts.
Inputs may be any that keep to these rules, and one draw needn't show every extreme that they name: `segment_ids`: ids never fall along the sequence; there are 4 documents, the longest exactly 640 positions.
All inputs are finite; a program needn't handle non-finite values.
Results may differ from a plain program's by a relative error of at most 0.02.
Values may be sent and summed in bfloat16 or wider, within the bound.
No kernel may reach another device: no remote copies, remote signals or barrier semaphores. Data moves between devices by JAX's collectives and lax.ppermute only.
A program may use at most 64 MiB of HBM per device.

v0:
```python
import math
import jax
import jax.numpy as jnp
from jax import lax
from jax.sharding import PartitionSpec as P

HD = 64
WINDOW = 128
neg_big = -1e30


def passed_along(value, axis, steps):
    count = lax.axis_size(axis)
    first, last = (max(0, -steps), min(count, count - steps))
    return lax.ppermute(value, axis, [(source, source + steps) for source in range(first, last)])


def shifted(block, axis, distance):
    devices = range(lax.axis_size(axis))
    route = [((i - distance) % len(devices), i) for i in devices]
    return lax.ppermute(block, axis, route)


def score_block(queries, key_block, score_scale):
    return (
        jnp.einsum("qgjd,kgd->gjqk", queries, key_block, preferred_element_type=jnp.float32)
        * score_scale
    )


def fold_block(running, queries, key_block, value_block, visible, score_scale):
    run_max, run_sum, weighted = running
    scores = jnp.where(visible[None, None], score_block(queries, key_block, score_scale), neg_big)
    new_max = jnp.maximum(run_max, jnp.max(scores, axis=-1))
    factor = jnp.exp(run_max - new_max)
    weights = jnp.exp(scores - new_max[..., None])
    run_sum = run_sum * factor + jnp.sum(weights, axis=-1)
    weighted = weighted * factor[..., None] + jnp.einsum(
        "gjqk,kgd->gjqd",
        weights.astype(jnp.bfloat16),
        value_block,
        preferred_element_type=jnp.float32,
    )
    return (new_max, run_sum, weighted)


def grad_core(weights, queries, grad_heads, key_block, value_block, row_delta, score_scale):
    grad_weights = jnp.einsum(
        "qgjd,kgd->gjqk", grad_heads, value_block, preferred_element_type=jnp.float32
    )
    grad_scores = weights * (grad_weights - row_delta[..., None])
    weights_low = weights.astype(jnp.bfloat16)
    scores_low = grad_scores.astype(jnp.bfloat16)
    value_grad = jnp.einsum(
        "gjqk,qgjd->kgd", weights_low, grad_heads, preferred_element_type=jnp.float32
    )
    key_grad = (
        jnp.einsum("gjqk,qgjd->kgd", scores_low, queries, preferred_element_type=jnp.float32)
        * score_scale
    )
    query_grad = (
        jnp.einsum("gjqk,kgd->qgjd", scores_low, key_block, preferred_element_type=jnp.float32)
        * score_scale
    )
    return (query_grad, key_grad, value_grad)


def output_delta(grad_heads, attended):
    return jnp.sum(jnp.transpose(grad_heads.astype(jnp.float32), (1, 2, 0, 3)) * attended, axis=-1)


def window_layer(
    segment_ids, query_rows, key_rows, value_rows, grad_rows, sink_logits, score_scale
):
    local_rows = query_rows.shape[0]
    key_cols = key_rows.shape[1]
    groups = key_cols // HD
    window_rows = WINDOW
    tail_keys = key_rows[local_rows - window_rows :]
    tail_values = value_rows[local_rows - window_rows :]
    tail_segs = segment_ids[local_rows - window_rows :]
    halo_keys, halo_values, halo_segs = passed_along((tail_keys, tail_values, tail_segs), "seq", 1)
    first_row = lax.axis_index("seq") * local_rows
    seen_keys = jnp.concatenate([halo_keys, key_rows], axis=0).reshape(
        local_rows + window_rows, groups, HD
    )
    seen_values = jnp.concatenate([halo_values, value_rows], axis=0).reshape(
        local_rows + window_rows, groups, HD
    )
    seen_segs = jnp.concatenate([halo_segs, segment_ids], axis=0)
    key_pos = first_row - window_rows + jnp.arange(local_rows + window_rows)
    query_pos = first_row + jnp.arange(local_rows)
    distance = query_pos[:, None] - key_pos[None, :]
    visible = (
        (distance >= 0)
        & (distance < window_rows)
        & (key_pos[None, :] >= 0)
        & (segment_ids[:, None] == seen_segs[None, :])
    )
    queries = query_rows.reshape(local_rows, groups, -1, HD)
    grad_heads = grad_rows.reshape(local_rows, groups, -1, HD)
    scores = jnp.where(visible[None, None], score_block(queries, seen_keys, score_scale), neg_big)
    sink_rows = sink_logits[:, :, None]
    row_max = jnp.maximum(jnp.max(scores, axis=-1), sink_rows)
    denominator = jnp.sum(jnp.exp(scores - row_max[..., None]), axis=-1) + jnp.exp(
        sink_rows - row_max
    )
    log_total = row_max + jnp.log(denominator)
    weights = jnp.where(visible[None, None], jnp.exp(scores - log_total[..., None]), 0.0)
    attended = jnp.einsum(
        "gjqk,kgd->gjqd",
        weights.astype(jnp.bfloat16),
        seen_values,
        preferred_element_type=jnp.float32,
    )
    row_delta = output_delta(grad_heads, attended)
    query_grad, key_grad, value_grad = grad_core(
        weights, queries, grad_heads, seen_keys, seen_values, row_delta, score_scale
    )
    key_grad = key_grad.reshape(local_rows + window_rows, key_cols)
    value_grad = value_grad.reshape(local_rows + window_rows, key_cols)
    back_keys, back_values = (
        passed_along(key_grad[:window_rows].astype(jnp.bfloat16), "seq", -1).astype(jnp.float32),
        passed_along(value_grad[:window_rows].astype(jnp.bfloat16), "seq", -1).astype(jnp.float32),
    )
    own_keys = key_grad[window_rows:]
    own_values = value_grad[window_rows:]
    split_at = local_rows - window_rows
    own_keys = jnp.concatenate([own_keys[:split_at], own_keys[split_at:] + back_keys], axis=0)
    own_values = jnp.concatenate(
        [own_values[:split_at], own_values[split_at:] + back_values], axis=0
    )
    return (query_grad.reshape(local_rows, groups, -1).astype(jnp.bfloat16), own_keys, own_values)


def body(
    segment_ids,
    window_query,
    window_keys,
    window_values,
    window_grad_out,
    window_sinks,
    full_query,
    full_keys,
    full_values,
    full_grad_out,
    full_sinks,
):
    score_scale = 1.0 / math.sqrt(HD)
    window_dq, window_kpart, window_vpart = window_layer(
        segment_ids,
        window_query,
        window_keys,
        window_values,
        window_grad_out,
        window_sinks,
        score_scale,
    )
    local_rows = full_query.shape[0]
    key_cols = full_keys.shape[1]
    groups = key_cols // HD
    seq_index = lax.axis_index("seq")
    seq_count = lax.axis_size("seq")
    query_pos = seq_index * local_rows + jnp.arange(local_rows)
    queries = full_query.reshape(local_rows, groups, -1, HD)
    grad_heads = full_grad_out.reshape(local_rows, groups, -1, HD)
    heads_per = queries.shape[2]
    sink_rows = jnp.broadcast_to(full_sinks[:, :, None], (groups, heads_per, local_rows))
    start_state = (
        sink_rows,
        jnp.ones_like(sink_rows),
        jnp.zeros((groups, heads_per, local_rows, HD), jnp.float32),
    )
    running = start_state
    first_row = jnp.int32(0)
    key_piece = lax.all_gather(full_keys, "seq", axis=0, tiled=True)
    value_piece = lax.all_gather(full_values, "seq", axis=0, tiled=True)
    seg_piece = lax.all_gather(segment_ids, "seq", axis=0, tiled=True)
    key_count = key_piece.shape[0]
    sub_rows = math.gcd(key_count, 512)
    for offset in range(0, key_count, sub_rows):
        key_block = key_piece[offset : offset + sub_rows].reshape(sub_rows, groups, HD)
        value_block = value_piece[offset : offset + sub_rows].reshape(sub_rows, groups, HD)
        seg_block = seg_piece[offset : offset + sub_rows]
        key_pos = first_row + offset + jnp.arange(sub_rows)
        visible = (query_pos[:, None] >= key_pos[None, :]) & (
            segment_ids[:, None] == seg_block[None, :]
        )
        previous = running
        running = fold_block(previous, queries, key_block, value_block, visible, score_scale)
    run_max, run_sum, weighted = running
    log_total = run_max + jnp.log(run_sum)
    row_delta = output_delta(grad_heads, weighted / run_sum[..., None])

    def contribution(source, keys_now, values_now, segs_now):
        key_pos = source * local_rows + jnp.arange(local_rows)
        visible = (query_pos[:, None] >= key_pos[None, :]) & (
            segment_ids[:, None] == segs_now[None, :]
        )
        key_block = keys_now.reshape(local_rows, groups, HD)
        value_block = values_now.reshape(local_rows, groups, HD)
        scores = score_block(queries, key_block, score_scale)
        weights = jnp.where(visible[None, None], jnp.exp(scores - log_total[..., None]), 0.0)
        query_grad, key_grad, value_grad = grad_core(
            weights, queries, grad_heads, key_block, value_block, row_delta, score_scale
        )
        return (
            query_grad,
            key_grad.reshape(local_rows, key_cols),
            value_grad.reshape(local_rows, key_cols),
        )

    query_start = jnp.zeros(queries.shape, jnp.float32)

    def circle_turn(turn_index, circle_state):
        query_acc, keys_now, values_now, segs_now, acc_keys, acc_values = circle_state
        source = (seq_index - turn_index) % seq_count
        query_part, key_part, value_part = contribution(source, keys_now, values_now, segs_now)
        keys_now, values_now, segs_now = passed_along((keys_now, values_now, segs_now), "seq", 1)
        acc_keys, acc_values = (
            shifted((acc_keys + key_part).astype(jnp.bfloat16), "seq", 1).astype(jnp.float32),
            shifted((acc_values + value_part).astype(jnp.bfloat16), "seq", 1).astype(jnp.float32),
        )
        return (query_acc + query_part, keys_now, values_now, segs_now, acc_keys, acc_values)

    zero_acc = jnp.zeros((local_rows, key_cols), jnp.float32)
    circle_state = (query_start, full_keys, full_values, segment_ids, zero_acc, zero_acc)
    query_acc, keys_now, values_now, segs_now, acc_keys, acc_values = lax.fori_loop(
        0, seq_count, circle_turn, circle_state
    )
    window_ksum, window_vsum, full_ksum, full_vsum = (
        lax.psum(window_kpart.astype(jnp.bfloat16), "rep").astype(jnp.float32),
        lax.psum(window_vpart.astype(jnp.bfloat16), "rep").astype(jnp.float32),
        lax.psum(acc_keys.astype(jnp.bfloat16), "rep").astype(jnp.float32),
        lax.psum(acc_values.astype(jnp.bfloat16), "rep").astype(jnp.float32),
    )
    full_dq = query_acc.reshape(local_rows, groups, -1).astype(jnp.bfloat16)
    return (
        window_dq,
        window_ksum.astype(jnp.bfloat16),
        window_vsum.astype(jnp.bfloat16),
        full_dq,
        full_ksum.astype(jnp.bfloat16),
        full_vsum.astype(jnp.bfloat16),
    )


def solution(mesh):
    placed = (
        P(("groups", "seq")),
        P(("groups", "seq"), "head", "rep"),
        P(("groups", "seq"), "head"),
        P(("groups", "seq"), "head"),
        P(("groups", "seq"), "head", "rep"),
        P("head", "rep"),
        P(("groups", "seq"), "head", "rep"),
        P(("groups", "seq"), "head"),
        P(("groups", "seq"), "head"),
        P(("groups", "seq"), "head", "rep"),
        P("head", "rep"),
    )
    return jax.shard_map(
        body,
        mesh=mesh,
        in_specs=placed,
        out_specs=(
            P(("groups", "seq"), "head", "rep"),
            P(("groups", "seq"), "head"),
            P(("groups", "seq"), "head"),
            P(("groups", "seq"), "head", "rep"),
            P(("groups", "seq"), "head"),
            P(("groups", "seq"), "head"),
        ),
        check_vma=False,
    )
```

profile of v0, /device:TPU:0, one launch (start us, length us, event | category | flops | bytes accessed | tf_op | source)
XLA Modules:
  0.0 240.3 jit_solution(12734191691278870327)
XLA Ops:
  7.3 17.6 %all_gather.10 = bf16[1024,256]{1,0:T(8,128)(2,1)S(1)} all-gather(bf16[256,256]{1,0:T(8,128)(2,1)} %param.20), channel_id=1, replica_groups=mesh['groups'=2,'seq'=4,'head'=2,'rep'=2] {'seq'}, dimensions={0}, use_global_device_ids=true | all-gather | bytes 655360 | tf_op jit(solution)/shard_map/all_gather | solution.py:176
  25.8 16.6 %all_gather.11 = bf16[1024,256]{1,0:T(8,128)(2,1)S(1)} all-gather(bf16[256,256]{1,0:T(8,128)(2,1)} %param.21), channel_id=1, replica_groups=mesh['groups'=2,'seq'=4,'head'=2,'rep'=2] {'seq'}, dimensions={0}, use_global_device_ids=true | all-gather | bytes 655360 | tf_op jit(solution)/shard_map/all_gather | solution.py:177
  45.9 10.6 %all-gather = s32[4,1,256]{2,1,0:T(1,128)S(1)} all-gather(s32[1,1,256]{2,1,0:T(1,128)} %bitcast.254), channel_id=1, replica_groups=mesh['groups'=2,'seq'=4,'head'=2,'rep'=2] {'seq'}, dimensions={0}, use_global_device_ids=true | all-gather | bytes 5120 | tf_op jit(solution)/shard_map/all_gather | solution.py:178
  64.4 2.1 copy.100
  70.4 3.8 %fusion.18 = (f32[4,4,256]{2,1,0:T(4,128)S(1)}, f32[4,4,256]{2,1,0:T(4,128)S(1)}) fusion(f32[4,512,256,4]{2,1,3,0:T(8,128)S(1)} %get-tuple-element.506, f32[4,4,256]{2,1,0:T(4,128)S(1)} %get-tuple-element.483, pred[256,512]{0,1:T(8,128)(4,1)S(1)} %get-tuple-element.498, f32[4,4,256]{2,1,0:T(4,128)S(1)} %max.50, ...), kind=kLoop, calls=%fused_computation.29 | loop fusion | flops 16769024 | bytes 17104896 | tf_op jit(solution)/shard_map/reduce_sum | solution.py:37
  74.4 2.1 fusion.39
  76.5 3.2 %fusion.46 = f32[4,4,256]{2,1,0:T(4,128)S(1)} fusion(bf16[256,4,4,64]{0,3,2,1:T(8,128)(2,1)} %bitcast.42, f32[4,4,256,64]{2,3,1,0:T(8,128)S(1)} %fusion.39, bf16[512,4,64,1]{0,2,3,1:T(8,128)(2,1)S(1)} %bitcast.246, f32[4,512,256,4]{2,1,3,0:T(8,128)S(1)} %get-tuple-element.508, f32[4,4,256]{2,1,0:T(4,128)S(1)} %max.50, ...), kind=kOutput, calls=%fused_computation.58 | convolution fusion | flops 278130688 | bytes 10403840 | tf_op jit(solution)/shard_map/gjqk,kgd->gjqd/dot_general | solution.py:38
  79.8 86.5 %while.26 = (s32[]{:T(128)}, f32[256,4,4,64]{0,3,2,1:T(8,128)S(1)}, bf16[256,256]{0,1:T(8,128)(2,1)S(1)}, bf16[256,256]{0,1:T(8,128)(2,1)S(1)}, s32[256]{0:T(256...) while((s32[]{:T(128)}, f32[256,4,4,64]{0,3,2,1:T(8,128)S(1)}, ...), condition=%wide.region_11.12_spmd.clone, body=%wide.region_10.11_spmd.clone.sunk | while | flops 683147776 | bytes 28963340 | solution.py:228
  79.8 1.4 collective-permute-start
  81.3 2.7 %collective-permute-start.1 = (bf16[256,256]{0,1:T(8,128)(2,1)S(1)}, bf16[256,256]{0,1:T(8,128)(2,1)S(1)}, u32[]{:S(2)}, u32[]{:S(2)}) collective-permute-start(bf16[256,256]{0,1:T(8,128)(2,1)S(1)} %copy.142), channel_id=1, source_target_pairs={{0,4},{4,8},{8,12},{1,5},{5,9},{9,13},{2,6},{6,10},{10,14},{3,7},{... | collective-permute-start | bytes 393224 | tf_op jit(solution)/shard_map/while/body/eval_jaxpr/ppermute | solution.py:15
  84.0 2.6 %collective-permute-start.2 = (s32[256]{0:T(256)S(1)}, s32[256]{0:T(256)S(1)}, u32[]{:S(2)}, u32[]{:S(2)}) collective-permute-start(s32[256]{0:T(256)S(1)} %copy.143), channel_id=1, source_target_pairs={{0,4},{4,8},{8,12},{1,5},{5,9},{9,13},{2,6},{6,10},{10,14},{3,7},{... | collective-permute-start | bytes 3080 | tf_op jit(solution)/shard_map/while/body/eval_jaxpr/ppermute | solution.py:15
  87.5 2.4 %fusion.121 = bf16[4,4,256,256]{2,3,1,0:T(8,128)(2,1)S(1)} fusion(f32[4,256,256,4]{2,1,3,0:T(8,128)S(1)} %fusion.120, bf16[256,4,64,1]{0,2,3,1:T(8,128)(2,1)S(1)} %bitcast.234, bf16[256,4,4,64]{0,3,2,1:T(8,128)(2,1)} %get-tuple-element.645, f32[4,4,256]{2,1,0:T(4,128)S(1)} %get-tuple-element.646, f32[4,4,256]{2,1,0:T(4,128)S(1)} %get-tuple-element.644, ...), kind=kOutput, calls=%fused_computation.3.clone.1 | convolution fusion | flops 140509184 | bytes 7045120 | tf_op jit(solution)/shard_map/while/body/eval_jaxpr/qgjd,kgd->gjqk/dot_general | solution.py:48
  90.8 1.9 fusion.125
  93.4 4.2 %collective-permute-done.3 = bf16[256,256]{0,1:T(8,128)(2,1)S(1)} collective-permute-done((bf16[256,256]{0,1:T(8,128)(2,1)S(1)}, bf16[256,256]{0,1:T(8,128)(2,1)S(1)}, u32[]{:S(2)}, u32[]{:S(2)}) %collective-permute-start.3) | collective-permute-done | bytes 131104 | tf_op jit(solution)/shard_map/while/body/eval_jaxpr/ppermute | solution.py:21
  97.6 2.0 collective-permute-done.4
  101.1 3.6 %collective-permute-start.1 = (bf16[256,256]{0,1:T(8,128)(2,1)S(1)}, bf16[256,256]{0,1:T(8,128)(2,1)S(1)}, u32[]{:S(2)}, u32[]{:S(2)}) collective-permute-start(bf16[256,256]{0,1:T(8,128)(2,1)S(1)} %copy.142), channel_id=1, source_target_pairs={{0,4},{4,8},{8,12},{1,5},{5,9},{9,13},{2,6},{6,10},{10,14},{3,7},{... | collective-permute-start | bytes 393224 | tf_op jit(solution)/shard_map/while/body/eval_jaxpr/ppermute | solution.py:15
  104.8 4.4 %collective-permute-start.2 = (s32[256]{0:T(256)S(1)}, s32[256]{0:T(256)S(1)}, u32[]{:S(2)}, u32[]{:S(2)}) collective-permute-start(s32[256]{0:T(256)S(1)} %copy.143), channel_id=1, source_target_pairs={{0,4},{4,8},{8,12},{1,5},{5,9},{9,13},{2,6},{6,10},{10,14},{3,7},{... | collective-permute-start | bytes 3080 | tf_op jit(solution)/shard_map/while/body/eval_jaxpr/ppermute | solution.py:15
  110.1 2.4 %fusion.121 = bf16[4,4,256,256]{2,3,1,0:T(8,128)(2,1)S(1)} fusion(f32[4,256,256,4]{2,1,3,0:T(8,128)S(1)} %fusion.120, bf16[256,4,64,1]{0,2,3,1:T(8,128)(2,1)S(1)} %bitcast.234, bf16[256,4,4,64]{0,3,2,1:T(8,128)(2,1)} %get-tuple-element.645, f32[4,4,256]{2,1,0:T(4,128)S(1)} %get-tuple-element.646, f32[4,4,256]{2,1,0:T(4,128)S(1)} %get-tuple-element.644, ...), kind=kOutput, calls=%fused_computation.3.clone.1 | convolution fusion | flops 140509184 | bytes 7045120 | tf_op jit(solution)/shard_map/while/body/eval_jaxpr/qgjd,kgd->gjqk/dot_general | solution.py:48
  113.4 1.9 fusion.125
  116.0 4.2 %collective-permute-done.3 = bf16[256,256]{0,1:T(8,128)(2,1)S(1)} collective-permute-done((bf16[256,256]{0,1:T(8,128)(2,1)S(1)}, bf16[256,256]{0,1:T(8,128)(2,1)S(1)}, u32[]{:S(2)}, u32[]{:S(2)}) %collective-permute-start.3) | collective-permute-done | bytes 131104 | tf_op jit(solution)/shard_map/while/body/eval_jaxpr/ppermute | solution.py:21
  120.2 2.0 collective-permute-done.4
  123.6 3.2 %collective-permute-start.1 = (bf16[256,256]{0,1:T(8,128)(2,1)S(1)}, bf16[256,256]{0,1:T(8,128)(2,1)S(1)}, u32[]{:S(2)}, u32[]{:S(2)}) collective-permute-start(bf16[256,256]{0,1:T(8,128)(2,1)S(1)} %copy.142), channel_id=1, source_target_pairs={{0,4},{4,8},{8,12},{1,5},{5,9},{9,13},{2,6},{6,10},{10,14},{3,7},{... | collective-permute-start | bytes 393224 | tf_op jit(solution)/shard_map/while/body/eval_jaxpr/ppermute | solution.py:15
  126.8 4.3 %collective-permute-start.2 = (s32[256]{0:T(256)S(1)}, s32[256]{0:T(256)S(1)}, u32[]{:S(2)}, u32[]{:S(2)}) collective-permute-start(s32[256]{0:T(256)S(1)} %copy.143), channel_id=1, source_target_pairs={{0,4},{4,8},{8,12},{1,5},{5,9},{9,13},{2,6},{6,10},{10,14},{3,7},{... | collective-permute-start | bytes 3080 | tf_op jit(solution)/shard_map/while/body/eval_jaxpr/ppermute | solution.py:15
  132.1 2.4 %fusion.121 = bf16[4,4,256,256]{2,3,1,0:T(8,128)(2,1)S(1)} fusion(f32[4,256,256,4]{2,1,3,0:T(8,128)S(1)} %fusion.120, bf16[256,4,64,1]{0,2,3,1:T(8,128)(2,1)S(1)} %bitcast.234, bf16[256,4,4,64]{0,3,2,1:T(8,128)(2,1)} %get-tuple-element.645, f32[4,4,256]{2,1,0:T(4,128)S(1)} %get-tuple-element.646, f32[4,4,256]{2,1,0:T(4,128)S(1)} %get-tuple-element.644, ...), kind=kOutput, calls=%fused_computation.3.clone.1 | convolution fusion | flops 140509184 | bytes 7045120 | tf_op jit(solution)/shard_map/while/body/eval_jaxpr/qgjd,kgd->gjqk/dot_general | solution.py:48
  135.4 1.9 fusion.125
  138.0 4.2 %collective-permute-done.3 = bf16[256,256]{0,1:T(8,128)(2,1)S(1)} collective-permute-done((bf16[256,256]{0,1:T(8,128)(2,1)S(1)}, bf16[256,256]{0,1:T(8,128)(2,1)S(1)}, u32[]{:S(2)}, u32[]{:S(2)}) %collective-permute-start.3) | collective-permute-done | bytes 131104 | tf_op jit(solution)/shard_map/while/body/eval_jaxpr/ppermute | solution.py:21
  142.2 2.0 collective-permute-done.4
  145.6 3.2 %collective-permute-start.1 = (bf16[256,256]{0,1:T(8,128)(2,1)S(1)}, bf16[256,256]{0,1:T(8,128)(2,1)S(1)}, u32[]{:S(2)}, u32[]{:S(2)}) collective-permute-start(bf16[256,256]{0,1:T(8,128)(2,1)S(1)} %copy.142), channel_id=1, source_target_pairs={{0,4},{4,8},{8,12},{1,5},{5,9},{9,13},{2,6},{6,10},{10,14},{3,7},{... | collective-permute-start | bytes 393224 | tf_op jit(solution)/shard_map/while/body/eval_jaxpr/ppermute | solution.py:15
  148.8 4.3 %collective-permute-start.2 = (s32[256]{0:T(256)S(1)}, s32[256]{0:T(256)S(1)}, u32[]{:S(2)}, u32[]{:S(2)}) collective-permute-start(s32[256]{0:T(256)S(1)} %copy.143), channel_id=1, source_target_pairs={{0,4},{4,8},{8,12},{1,5},{5,9},{9,13},{2,6},{6,10},{10,14},{3,7},{... | collective-permute-start | bytes 3080 | tf_op jit(solution)/shard_map/while/body/eval_jaxpr/ppermute | solution.py:15
  154.1 2.4 %fusion.121 = bf16[4,4,256,256]{2,3,1,0:T(8,128)(2,1)S(1)} fusion(f32[4,256,256,4]{2,1,3,0:T(8,128)S(1)} %fusion.120, bf16[256,4,64,1]{0,2,3,1:T(8,128)(2,1)S(1)} %bitcast.234, bf16[256,4,4,64]{0,3,2,1:T(8,128)(2,1)} %get-tuple-element.645, f32[4,4,256]{2,1,0:T(4,128)S(1)} %get-tuple-element.646, f32[4,4,256]{2,1,0:T(4,128)S(1)} %get-tuple-element.644, ...), kind=kOutput, calls=%fused_computation.3.clone.1 | convolution fusion | flops 140509184 | bytes 7045120 | tf_op jit(solution)/shard_map/while/body/eval_jaxpr/qgjd,kgd->gjqk/dot_general | solution.py:48
  157.4 1.9 fusion.125
  160.0 4.2 %collective-permute-done.3 = bf16[256,256]{0,1:T(8,128)(2,1)S(1)} collective-permute-done((bf16[256,256]{0,1:T(8,128)(2,1)S(1)}, bf16[256,256]{0,1:T(8,128)(2,1)S(1)}, u32[]{:S(2)}, u32[]{:S(2)}) %collective-permute-start.3) | collective-permute-done | bytes 131104 | tf_op jit(solution)/shard_map/while/body/eval_jaxpr/ppermute | solution.py:21
  164.2 2.0 collective-permute-done.4
  167.6 3.2 %collective-permute-start.5 = (bf16[128,256]{1,0:T(8,128)(2,1)S(1)}, bf16[128,256]{1,0:T(8,128)(2,1)S(1)}, u32[]{:S(2)}, u32[]{:S(2)}) collective-permute-start(bf16[128,256]{1,0:T(8,128)(2,1)S(1)} %slice.71), channel_id=1, source_target_pairs={{0,4},{4,8},{8,12},{1,5},{5,9},{9,13},{2,6},{6,10},{10,14},{3,7},{... | collective-permute-start | bytes 196616 | tf_op jit(solution)/shard_map/ppermute | solution.py:15
  170.8 4.6 %collective-permute-start.7 = (bf16[128,256]{1,0:T(8,128)(2,1)S(1)}, bf16[128,256]{1,0:T(8,128)(2,1)S(1)}, u32[]{:S(2)}, u32[]{:S(2)}) collective-permute-start(bf16[128,256]{1,0:T(8,128)(2,1)S(1)} %slice.73), channel_id=1, source_target_pairs={{0,4},{4,8},{8,12},{1,5},{5,9},{9,13},{2,6},{6,10},{10,14},{3,7},{... | collective-permute-start | bytes 196616 | tf_op jit(solution)/shard_map/ppermute | solution.py:15
  178.3 1.5 copy.86
  182.9 2.5 %fusion.66 = (bf16[384,4,64]{0,2,1:T(8,128)(2,1)S(1)}, f32[384,4,64]{0,2,1:T(8,128)}) fusion(bf16[256,4,4,64]{0,3,2,1:T(8,128)(2,1)S(1)} %bitcast.241, f32[4,384,256,4]{2,1,3,0:T(8,128)S(1)} %get-tuple-element.500, f32[4,4,256]{2,1,0:T(4,128)S(1)} %log_add_fusion.1, pred[256,384]{0,1:T(8,128)(4,1)S(1)} %fusion.52), kind=kOutput, calls=%fused_computation.96 | convolution fusion | flops 209289216 | bytes 7520256 | tf_op jit(solution)/shard_map/gjqk,qgjd->kgd/dot_general | solution.py:54
  188.2 1.9 copy.85
  190.1 4.8 %fusion.43 = f32[4,4,256]{2,1,0:T(4,128)S(1)} fusion(bf16[384,4,64,1]{0,2,3,1:T(8,128)(2,1)} %bitcast.252, bf16[256,4,4,64]{0,3,2,1:T(8,128)(2,1)} %bitcast.242, f32[4,384,256,4]{2,1,3,0:T(8,128)} %copy-done, f32[4,4,256]{2,1,0:T(4,128)S(1)} %log_add_fusion.1, pred[256,384]{0,1:T(8,128)(4,1)S(1)} %fusion.52), kind=kOutput, calls=%fused_computation.52 | convolution fusion | flops 209973248 | bytes 7143424 | tf_op jit(solution)/shard_map/gjqk,kgd->gjqd/dot_general | solution.py:110
  195.0 2.0 fusion.24
  197.0 1.6 copy-done.1
  204.1 3.7 %collective-permute-done.8 = bf16[128,256]{1,0:T(8,128)(2,1)S(1)} collective-permute-done((bf16[128,256]{1,0:T(8,128)(2,1)S(1)}, bf16[128,256]{1,0:T(8,128)(2,1)S(1)}, u32[]{:S(2)}, u32[]{:S(2)}) %collective-permute-start.8) | collective-permute-done | bytes 65568 | tf_op jit(solution)/shard_map/ppermute | solution.py:15
  209.6 2.6 %fusion.42 = bf16[4,64,4,256]{3,1,2,0:T(8,128)(2,1)S(1)} fusion(bf16[384,4,64,1]{0,2,3,1:T(8,128)(2,1)S(1)} %bitcast.237, bf16[4,4,256,384]{2,3,1,0:T(8,128)(2,1)} %copy-done.1), kind=kOutput, calls=%fused_computation.51 | convolution fusion | flops 201850880 | bytes 3866624 | tf_op jit(solution)/shard_map/gjqk,kgd->qgjd/dot_general | solution.py:62
  213.3 13.9 %all-reduce.3.cloned.1.call-done = (bf16[256,256]{1,0:T(8,128)(2,1)}, bf16[256,256]{1,0:T(8,128)(2,1)}, bf16[256,256]{1,0:T(8,128)(2,1)}, bf16[256,256]{1,0:T(8,128)(2,1)}) async-done(((bf16[256,256]{1,0:T(8,128)(2,1)}, bf16[256,256]{1,0:T(8,128)(2,1)}, bf16[256,256]{1,0:T(8,128)(2,1)}, bf16[256,256]{1,0:T(8,128)(2,1)}), (bf16[256,256]{1,0:T(8,128)(2,1)}, bf16[256,256]{1,0:T(8,128)(2,1)}, ...) | async-done | bytes 524304 | tf_op jit(solution)/shard_map/psum | solution.py:232
  227.1 1.6 copy.157
  228.7 1.6 copy.158
  230.3 1.6 copy.159
  231.8 1.6 copy.160
  (175 shorter events, 48.3 us)
Async XLA Ops:
  7.2 59.4 %copy-start.10 = (s32[256]{0:T(256)S(1)}, s32[256]{0:T(256)}, u32[]{:S(2)}) copy-start(s32[256]{0:T(256)} %param.13) | copy-start | bytes 3076
  7.2 220.0 %all-reduce.3.cloned.1.call-start = ((), (), s32[]{:S(2)}) async-start(), calls=%async_computation | async-start | bytes 1048576 | tf_op jit(solution)/shard_map/psum | solution.py:232
  67.5 1.4 copy-start.11
  79.7 86.5 %copy-start.14 = (s32[128]{0:T(128)S(1)}, s32[128]{0:T(128)}, u32[]{:S(2)}) copy-start(s32[128]{0:T(128)} %slice.72) | copy-start | bytes 1540
  79.7 87.8 %copy-start.6 = (bf16[256,256]{1,0:T(8,128)(2,1)S(1)}, bf16[256,256]{1,0:T(8,128)(2,1)}, u32[]{:S(2)}) copy-start(bf16[256,256]{1,0:T(8,128)(2,1)} %param.15) | copy-start | bytes 393220
  79.8 91.1 %copy-start.7 = (bf16[256,256]{1,0:T(8,128)(2,1)S(1)}, bf16[256,256]{1,0:T(8,128)(2,1)}, u32[]{:S(2)}) copy-start(bf16[256,256]{1,0:T(8,128)(2,1)} %param.16) | copy-start | bytes 393220
  79.8 100.1 %copy-start.13 = (s32[256]{0:T(256)S(1)}, s32[256]{0:T(256)}, u32[]{:S(2)}) copy-start(s32[256]{0:T(256)} %iota_add_fusion.4) | copy-start | bytes 3076
  79.8 19.8 %collective-permute-start = (bf16[256,256]{0,1:T(8,128)(2,1)S(1)}, bf16[256,256]{0,1:T(8,128)(2,1)S(1)}, u32[]{:S(2)}, u32[]{:S(2)}) collective-permute-start(bf16[256,256]{0,1:T(8,128)(2,1)S(1)} %copy.141), channel_id=1, source_target_pairs={{0,4},{4,8},{8,12},{1,5},{5,9},{9,13},{2,6},{6,10},{10,14},{3,7},{... | collective-permute-start | bytes 393224 | tf_op jit(solution)/shard_map/while/body/eval_jaxpr/ppermute | solution.py:15
  81.3 18.4 %collective-permute-start.1 = (bf16[256,256]{0,1:T(8,128)(2,1)S(1)}, bf16[256,256]{0,1:T(8,128)(2,1)S(1)}, u32[]{:S(2)}, u32[]{:S(2)}) collective-permute-start(bf16[256,256]{0,1:T(8,128)(2,1)S(1)} %copy.142), channel_id=1, source_target_pairs={{0,4},{4,8},{8,12},{1,5},{5,9},{9,13},{2,6},{6,10},{10,14},{3,7},{... | collective-permute-start | bytes 393224 | tf_op jit(solution)/shard_map/while/body/eval_jaxpr/ppermute | solution.py:15
  84.0 15.6 %collective-permute-start.2 = (s32[256]{0:T(256)S(1)}, s32[256]{0:T(256)S(1)}, u32[]{:S(2)}, u32[]{:S(2)}) collective-permute-start(s32[256]{0:T(256)S(1)} %copy.143), channel_id=1, source_target_pairs={{0,4},{4,8},{8,12},{1,5},{5,9},{9,13},{2,6},{6,10},{10,14},{3,7},{... | collective-permute-start | bytes 3080 | tf_op jit(solution)/shard_map/while/body/eval_jaxpr/ppermute | solution.py:15
  90.8 6.8 %collective-permute-start.3 = (bf16[256,256]{0,1:T(8,128)(2,1)S(1)}, bf16[256,256]{0,1:T(8,128)(2,1)S(1)}, u32[]{:S(2)}, u32[]{:S(2)}) collective-permute-start(bf16[256,256]{0,1:T(8,128)(2,1)S(1)} %fusion.124), channel_id=1, source_target_pairs={{12,0},{0,4},{4,8},{8,12},{13,1},{1,5},{5,9},{9,13},{14,2},{2,6},{... | collective-permute-start | bytes 393224 | tf_op jit(solution)/shard_map/while/body/eval_jaxpr/ppermute | solution.py:21
  92.8 6.8 %collective-permute-start.4 = (bf16[256,256]{0,1:T(8,128)(2,1)S(1)}, bf16[256,256]{0,1:T(8,128)(2,1)S(1)}, u32[]{:S(2)}, u32[]{:S(2)}) collective-permute-start(bf16[256,256]{0,1:T(8,128)(2,1)S(1)} %fusion.126), channel_id=1, source_target_pairs={{12,0},{0,4},{4,8},{8,12},{13,1},{1,5},{5,9},{9,13},{14,2},{2,6},{... | collective-permute-start | bytes 393224 | tf_op jit(solution)/shard_map/while/body/eval_jaxpr/ppermute | solution.py:21
  99.7 22.5 %collective-permute-start = (bf16[256,256]{0,1:T(8,128)(2,1)S(1)}, bf16[256,256]{0,1:T(8,128)(2,1)S(1)}, u32[]{:S(2)}, u32[]{:S(2)}) collective-permute-start(bf16[256,256]{0,1:T(8,128)(2,1)S(1)} %copy.141), channel_id=1, source_target_pairs={{0,4},{4,8},{8,12},{1,5},{5,9},{9,13},{2,6},{6,10},{10,14},{3,7},{... | collective-permute-start | bytes 393224 | tf_op jit(solution)/shard_map/while/body/eval_jaxpr/ppermute | solution.py:15
  101.1 21.1 %collective-permute-start.1 = (bf16[256,256]{0,1:T(8,128)(2,1)S(1)}, bf16[256,256]{0,1:T(8,128)(2,1)S(1)}, u32[]{:S(2)}, u32[]{:S(2)}) collective-permute-start(bf16[256,256]{0,1:T(8,128)(2,1)S(1)} %copy.142), channel_id=1, source_target_pairs={{0,4},{4,8},{8,12},{1,5},{5,9},{9,13},{2,6},{6,10},{10,14},{3,7},{... | collective-permute-start | bytes 393224 | tf_op jit(solution)/shard_map/while/body/eval_jaxpr/ppermute | solution.py:15
  104.8 17.4 %collective-permute-start.2 = (s32[256]{0:T(256)S(1)}, s32[256]{0:T(256)S(1)}, u32[]{:S(2)}, u32[]{:S(2)}) collective-permute-start(s32[256]{0:T(256)S(1)} %copy.143), channel_id=1, source_target_pairs={{0,4},{4,8},{8,12},{1,5},{5,9},{9,13},{2,6},{6,10},{10,14},{3,7},{... | collective-permute-start | bytes 3080 | tf_op jit(solution)/shard_map/while/body/eval_jaxpr/ppermute | solution.py:15
  113.3 6.8 %collective-permute-start.3 = (bf16[256,256]{0,1:T(8,128)(2,1)S(1)}, bf16[256,256]{0,1:T(8,128)(2,1)S(1)}, u32[]{:S(2)}, u32[]{:S(2)}) collective-permute-start(bf16[256,256]{0,1:T(8,128)(2,1)S(1)} %fusion.124), channel_id=1, source_target_pairs={{12,0},{0,4},{4,8},{8,12},{13,1},{1,5},{5,9},{9,13},{14,2},{2,6},{... | collective-permute-start | bytes 393224 | tf_op jit(solution)/shard_map/while/body/eval_jaxpr/ppermute | solution.py:21
  115.4 6.8 %collective-permute-start.4 = (bf16[256,256]{0,1:T(8,128)(2,1)S(1)}, bf16[256,256]{0,1:T(8,128)(2,1)S(1)}, u32[]{:S(2)}, u32[]{:S(2)}) collective-permute-start(bf16[256,256]{0,1:T(8,128)(2,1)S(1)} %fusion.126), channel_id=1, source_target_pairs={{12,0},{0,4},{4,8},{8,12},{13,1},{1,5},{5,9},{9,13},{14,2},{2,6},{... | collective-permute-start | bytes 393224 | tf_op jit(solution)/shard_map/while/body/eval_jaxpr/ppermute | solution.py:21
  122.3 22.0 %collective-permute-start = (bf16[256,256]{0,1:T(8,128)(2,1)S(1)}, bf16[256,256]{0,1:T(8,128)(2,1)S(1)}, u32[]{:S(2)}, u32[]{:S(2)}) collective-permute-start(bf16[256,256]{0,1:T(8,128)(2,1)S(1)} %copy.141), channel_id=1, source_target_pairs={{0,4},{4,8},{8,12},{1,5},{5,9},{9,13},{2,6},{6,10},{10,14},{3,7},{... | collective-permute-start | bytes 393224 | tf_op jit(solution)/shard_map/while/body/eval_jaxpr/ppermute | solution.py:15
  123.6 20.6 %collective-permute-start.1 = (bf16[256,256]{0,1:T(8,128)(2,1)S(1)}, bf16[256,256]{0,1:T(8,128)(2,1)S(1)}, u32[]{:S(2)}, u32[]{:S(2)}) collective-permute-start(bf16[256,256]{0,1:T(8,128)(2,1)S(1)} %copy.142), channel_id=1, source_target_pairs={{0,4},{4,8},{8,12},{1,5},{5,9},{9,13},{2,6},{6,10},{10,14},{3,7},{... | collective-permute-start | bytes 393224 | tf_op jit(solution)/shard_map/while/body/eval_jaxpr/ppermute | solution.py:15
  126.8 17.4 %collective-permute-start.2 = (s32[256]{0:T(256)S(1)}, s32[256]{0:T(256)S(1)}, u32[]{:S(2)}, u32[]{:S(2)}) collective-permute-start(s32[256]{0:T(256)S(1)} %copy.143), channel_id=1, source_target_pairs={{0,4},{4,8},{8,12},{1,5},{5,9},{9,13},{2,6},{6,10},{10,14},{3,7},{... | collective-permute-start | bytes 3080 | tf_op jit(solution)/shard_map/while/body/eval_jaxpr/ppermute | solution.py:15
  135.3 6.8 %collective-permute-start.3 = (bf16[256,256]{0,1:T(8,128)(2,1)S(1)}, bf16[256,256]{0,1:T(8,128)(2,1)S(1)}, u32[]{:S(2)}, u32[]{:S(2)}) collective-permute-start(bf16[256,256]{0,1:T(8,128)(2,1)S(1)} %fusion.124), channel_id=1, source_target_pairs={{12,0},{0,4},{4,8},{8,12},{13,1},{1,5},{5,9},{9,13},{14,2},{2,6},{... | collective-permute-start | bytes 393224 | tf_op jit(solution)/shard_map/while/body/eval_jaxpr/ppermute | solution.py:21
  137.4 6.8 %collective-permute-start.4 = (bf16[256,256]{0,1:T(8,128)(2,1)S(1)}, bf16[256,256]{0,1:T(8,128)(2,1)S(1)}, u32[]{:S(2)}, u32[]{:S(2)}) collective-permute-start(bf16[256,256]{0,1:T(8,128)(2,1)S(1)} %fusion.126), channel_id=1, source_target_pairs={{12,0},{0,4},{4,8},{8,12},{13,1},{1,5},{5,9},{9,13},{14,2},{2,6},{... | collective-permute-start | bytes 393224 | tf_op jit(solution)/shard_map/while/body/eval_jaxpr/ppermute | solution.py:21
  144.3 22.0 %collective-permute-start = (bf16[256,256]{0,1:T(8,128)(2,1)S(1)}, bf16[256,256]{0,1:T(8,128)(2,1)S(1)}, u32[]{:S(2)}, u32[]{:S(2)}) collective-permute-start(bf16[256,256]{0,1:T(8,128)(2,1)S(1)} %copy.141), channel_id=1, source_target_pairs={{0,4},{4,8},{8,12},{1,5},{5,9},{9,13},{2,6},{6,10},{10,14},{3,7},{... | collective-permute-start | bytes 393224 | tf_op jit(solution)/shard_map/while/body/eval_jaxpr/ppermute | solution.py:15
  145.6 20.6 %collective-permute-start.1 = (bf16[256,256]{0,1:T(8,128)(2,1)S(1)}, bf16[256,256]{0,1:T(8,128)(2,1)S(1)}, u32[]{:S(2)}, u32[]{:S(2)}) collective-permute-start(bf16[256,256]{0,1:T(8,128)(2,1)S(1)} %copy.142), channel_id=1, source_target_pairs={{0,4},{4,8},{8,12},{1,5},{5,9},{9,13},{2,6},{6,10},{10,14},{3,7},{... | collective-permute-start | bytes 393224 | tf_op jit(solution)/shard_map/while/body/eval_jaxpr/ppermute | solution.py:15
  148.8 17.4 %collective-permute-start.2 = (s32[256]{0:T(256)S(1)}, s32[256]{0:T(256)S(1)}, u32[]{:S(2)}, u32[]{:S(2)}) collective-permute-start(s32[256]{0:T(256)S(1)} %copy.143), channel_id=1, source_target_pairs={{0,4},{4,8},{8,12},{1,5},{5,9},{9,13},{2,6},{6,10},{10,14},{3,7},{... | collective-permute-start | bytes 3080 | tf_op jit(solution)/shard_map/while/body/eval_jaxpr/ppermute | solution.py:15
  157.3 6.8 %collective-permute-start.3 = (bf16[256,256]{0,1:T(8,128)(2,1)S(1)}, bf16[256,256]{0,1:T(8,128)(2,1)S(1)}, u32[]{:S(2)}, u32[]{:S(2)}) collective-permute-start(bf16[256,256]{0,1:T(8,128)(2,1)S(1)} %fusion.124), channel_id=1, source_target_pairs={{12,0},{0,4},{4,8},{8,12},{13,1},{1,5},{5,9},{9,13},{14,2},{2,6},{... | collective-permute-start | bytes 393224 | tf_op jit(solution)/shard_map/while/body/eval_jaxpr/ppermute | solution.py:21
  159.4 6.8 %collective-permute-start.4 = (bf16[256,256]{0,1:T(8,128)(2,1)S(1)}, bf16[256,256]{0,1:T(8,128)(2,1)S(1)}, u32[]{:S(2)}, u32[]{:S(2)}) collective-permute-start(bf16[256,256]{0,1:T(8,128)(2,1)S(1)} %fusion.126), channel_id=1, source_target_pairs={{12,0},{0,4},{4,8},{8,12},{13,1},{1,5},{5,9},{9,13},{14,2},{2,6},{... | collective-permute-start | bytes 393224 | tf_op jit(solution)/shard_map/while/body/eval_jaxpr/ppermute | solution.py:21
  166.3 15.1 %copy-start.12 = (f32[4,4]{1,0:T(4,128)S(1)}, f32[4,4]{1,0:T(4,128)}, u32[]{:S(2)}) copy-start(f32[4,4]{1,0:T(4,128)} %param.18) | copy-start | bytes 196
  166.3 13.6 %collective-permute-start.6 = (s32[128]{0:T(128)S(1)}, s32[128]{0:T(128)S(1)}, u32[]{:S(2)}, u32[]{:S(2)}) collective-permute-start(s32[128]{0:T(128)S(1)} %copy-done.14), channel_id=1, source_target_pairs={{0,4},{4,8},{8,12},{1,5},{5,9},{9,13},{2,6},{6,10},{10,14},{3,7},{... | collective-permute-start | bytes 1544 | tf_op jit(solution)/shard_map/ppermute | solution.py:15
  167.6 12.5 %collective-permute-start.5 = (bf16[128,256]{1,0:T(8,128)(2,1)S(1)}, bf16[128,256]{1,0:T(8,128)(2,1)S(1)}, u32[]{:S(2)}, u32[]{:S(2)}) collective-permute-start(bf16[128,256]{1,0:T(8,128)(2,1)S(1)} %slice.71), channel_id=1, source_target_pairs={{0,4},{4,8},{8,12},{1,5},{5,9},{9,13},{2,6},{6,10},{10,14},{3,7},{... | collective-permute-start | bytes 196616 | tf_op jit(solution)/shard_map/ppermute | solution.py:15
  170.8 16.7 %collective-permute-start.7 = (bf16[128,256]{1,0:T(8,128)(2,1)S(1)}, bf16[128,256]{1,0:T(8,128)(2,1)S(1)}, u32[]{:S(2)}, u32[]{:S(2)}) collective-permute-start(bf16[128,256]{1,0:T(8,128)(2,1)S(1)} %slice.73), channel_id=1, source_target_pairs={{0,4},{4,8},{8,12},{1,5},{5,9},{9,13},{2,6},{6,10},{10,14},{3,7},{... | collective-permute-start | bytes 196616 | tf_op jit(solution)/shard_map/ppermute | solution.py:15
  178.3 4.5 %copy-start.2 = (bf16[256,4,256]{0,2,1:T(8,128)(2,1)}, bf16[256,4,256]{0,2,1:T(8,128)(2,1)S(1)}, u32[]{:S(2)}) copy-start(bf16[256,4,256]{0,2,1:T(8,128)(2,1)S(1)} %copy.84) | copy-start | bytes 1572868
  179.8 3.1 %copy-start.4 = (bf16[256,4,256]{0,2,1:T(8,128)(2,1)}, bf16[256,4,256]{0,2,1:T(8,128)(2,1)S(1)}, u32[]{:S(2)}) copy-start(bf16[256,4,256]{0,2,1:T(8,128)(2,1)S(1)} %copy.86) | copy-start | bytes 1572868
  181.4 4.0 %copy-start = (f32[4,384,256,4]{2,1,3,0:T(8,128)}, f32[4,384,256,4]{2,1,3,0:T(8,128)S(1)}, u32[]{:S(2)}) copy-start(f32[4,384,256,4]{2,1,3,0:T(8,128)S(1)} %get-tuple-element.500) | copy-start | bytes 18874372
  182.9 4.6 %copy-start.8 = (bf16[256,256]{1,0:T(8,128)(2,1)S(1)}, bf16[256,256]{1,0:T(8,128)(2,1)}, u32[]{:S(2)}) copy-start(bf16[256,256]{1,0:T(8,128)(2,1)} %param.16) | copy-start | bytes 393220
  186.2 16.3 %collective-permute-start.9 = (bf16[128,256]{1,0:T(8,128)(2,1)}, bf16[128,256]{1,0:T(8,128)(2,1)}, u32[]{:S(2)}, u32[]{:S(2)}) collective-permute-start(bf16[128,256]{1,0:T(8,128)(2,1)} %copy.94), channel_id=1, source_target_pairs={{4,0},{8,4},{12,8},{5,1},{9,5},{13,9},{6,2},{10,6},{14,10},{7,3},{... | collective-permute-start | bytes 196616 | tf_op jit(solution)/shard_map/ppermute | solution.py:15
  188.2 6.7 %slice-start = ((s8[6291456]{0:T(1024)(128)(4,1)}), s8[2097152]{0:T(1024)(128)(4,1)S(1)}, s32[]{:S(2)}) async-start(s8[6291456]{0:T(1024)(128)(4,1)} %bitcast.230), calls=%async_computation.1 | async-start | bytes 4194304
  190.1 4.8 %copy-start.5 = (bf16[256,4,256]{0,2,1:T(8,128)(2,1)S(1)}, bf16[256,4,256]{0,2,1:T(8,128)(2,1)}, u32[]{:S(2)}) copy-start(bf16[256,4,256]{0,2,1:T(8,128)(2,1)} %copy-done.4) | copy-start | bytes 1572868
  190.1 4.8 %copy-start.9 = (bf16[384,256]{0,1:T(8,128)(2,1)S(1)}, bf16[384,256]{0,1:T(8,128)(2,1)}, u32[]{:S(2)}) copy-start(bf16[384,256]{0,1:T(8,128)(2,1)} %copy.85) | copy-start | bytes 589828
  190.1 4.8 %slice-start.1 = ((s8[6291456]{0:T(1024)(128)(4,1)}), s8[4194304]{0:T(1024)(128)(4,1)S(1)}, s32[]{:S(2)}) async-start(s8[6291456]{0:T(1024)(128)(4,1)} %bitcast.230), calls=%async_computation.2 | async-start | bytes 8388608
  195.0 3.7 %copy-start.3 = (bf16[256,4,256]{0,2,1:T(8,128)(2,1)S(1)}, bf16[256,4,256]{0,2,1:T(8,128)(2,1)}, u32[]{:S(2)}) copy-start(bf16[256,4,256]{0,2,1:T(8,128)(2,1)} %copy-done.2) | copy-start | bytes 1572868
  197.0 1.6 copy-start.1
  201.0 6.8 %collective-permute-start.8 = (bf16[128,256]{1,0:T(8,128)(2,1)S(1)}, bf16[128,256]{1,0:T(8,128)(2,1)S(1)}, u32[]{:S(2)}, u32[]{:S(2)}) collective-permute-start(bf16[128,256]{1,0:T(8,128)(2,1)S(1)} %copy.90), channel_id=1, source_target_pairs={{4,0},{8,4},{12,8},{5,1},{9,5},{13,9},{6,2},{10,6},{14,10},{7,3},{... | collective-permute-start | bytes 196616 | tf_op jit(solution)/shard_map/ppermute | solution.py:15
Sparse Core Ops, SparseCore 0:
  208.6 18.4 all-reduce.2
where the time goes:
time: 242 us; the launch traced here: 240 us
  matrix products  47.6 us (20%)
  starting transfers between devices  46.1 us (19%)
  blocking collectives  44.7 us (18%)
  waiting for transfers between devices  42.4 us (18%)
  local copies, waits for them, and re-layouts  32.8 us (14%)
  between operations  14.6 us (6%)
  other arithmetic  11.3 us (5%)
    ppermute x17, starting transfers between devices, passed_along(): lax.ppermute(value, axis, [(source, source + steps) for source in range(f...  45.5 us
    ppermute x8, waiting for transfers between devices, shifted(): return lax.ppermute(block, axis, route)  24.7 us
    unnamed x47, local copies, waits for them, and re-layouts  19 us
    all_gather x1, blocking collectives, body(): key_piece = lax.all_gather(full_keys, 'seq', axis=0, tiled=True)  17.6 us
    all_gather x1, blocking collectives, body(): value_piece = lax.all_gather(full_values, 'seq', axis=0, tiled=True)  16.6 us
    psum x1, waiting for transfers between devices, body(): lax.psum(window_kpart.astype(jnp.bfloat16), 'rep').astype(jnp.float32)  13.9 us
    dot_general x5, matrix products, grad_core(): jnp.einsum('qgjd,kgd->gjqk', grad_heads, value_block, preferred_element_t...  11.7 us
    all_gather x1, blocking collectives, body(): seg_piece = lax.all_gather(segment_ids, 'seq', axis=0, tiled=True)  10.6 us
  transfers between devices with their start and end apart: 26, of which 10 were waited for; matrix products, arithmetic and copies ran while one was open for 23% of the time, Pallas kernels for 0%

commit v1 on v0

--- a/solution.py
+++ b/solution.py
@@ -175,7 +175,12 @@
     first_row = jnp.int32(0)
     key_piece = lax.all_gather(full_keys, "seq", axis=0, tiled=True)
     value_piece = lax.all_gather(full_values, "seq", axis=0, tiled=True)
-    seg_piece = lax.all_gather(segment_ids, "seq", axis=0, tiled=True)
+    ring = [segment_ids]
+    for hop in range(3):
+        ring.append(lax.ppermute(ring[-1], "seq", [(dev, (dev + 1) % 4) for dev in range(4)]))
+    seg_piece = jnp.roll(
+        jnp.concatenate(ring[::-1], axis=0), (lax.axis_index("seq") + 1) * ring[0].shape[0], axis=0
+    )
     key_count = key_piece.shape[0]
     sub_rows = math.gcd(key_count, 512)
     for offset in range(0, key_count, sub_rows):

time: 242 us -> 233 us (0.963)
  blocking collectives: 44.7 us -> 31.1 us
  starting transfers between devices: 46.1 us -> 53.2 us
  local copies, waits for them, and re-layouts: 32.8 us -> 29.9 us
    all_gather x1 -> x0, blocking collectives: 10.6 us -> none  [body(): seg_piece = lax.all_gather(segment_ids, 'seq', axis=0, tiled=True)]
    ppermute x17, starting transfers between devices: 45.5 us -> 49.4 us  [passed_along(): lax.ppermute(value, axis, [(source, source + steps) for source in range(f...]
    ppermute x0 -> x3, starting transfers between devices: none -> 3.16 us  [body(): lax.ppermute(ring[-1], 'seq', [(dev, (dev + 1) % 4) for dev in range(4)])]
    slice x3, local copies, waits for them, and re-layouts: 3 us -> 0.32 us  [body(): key_piece[offset:offset + sub_rows].reshape(sub_rows, groups, HD)]
    unnamed x47 -> x54, local copies, waits for them, and re-layouts: 19 us -> 19.1 us
  transfers between devices with their start and end apart: 26 -> 29, of which waited for: 10 -> 11; matrix products, arithmetic and copies ran while one was open for 23% -> 29% of each run, Pallas kernels for 0% -> 0%
where the time goes in v1:
time: 233 us; the launch traced here: 232 us
  starting transfers between devices  53.2 us (23%)
  matrix products  47.6 us (20%)
  waiting for transfers between devices  43.7 us (19%)
  blocking collectives  31.1 us (13%)
  local copies, waits for them, and re-layouts  29.9 us (13%)
  between operations  14.6 us (6%)
  other arithmetic  10.9 us (5%)
    ppermute x17, starting transfers between devices, passed_along(): lax.ppermute(value, axis, [(source, source + steps) for source in range(f...  49.4 us
    ppermute x8, waiting for transfers between devices, shifted(): return lax.ppermute(block, axis, route)  24.7 us
    unnamed x54, local copies, waits for them, and re-layouts  19.1 us
    all_gather x1, blocking collectives, body(): key_piece = lax.all_gather(full_keys, 'seq', axis=0, tiled=True)  15.6 us
    all_gather x1, blocking collectives, body(): value_piece = lax.all_gather(full_values, 'seq', axis=0, tiled=True)  15.5 us
    psum x1, waiting for transfers between devices, body(): lax.psum(window_kpart.astype(jnp.bfloat16), 'rep').astype(jnp.float32)  13.8 us
    dot_general x5, matrix products, grad_core(): jnp.einsum('qgjd,kgd->gjqk', grad_heads, value_block, preferred_element_t...  11.7 us
    dot_general x5, matrix products, grad_core(): jnp.einsum('gjqk,qgjd->kgd', weights_low, grad_heads, preferred_element_t...  10.2 us
  transfers between devices with their start and end apart: 29, of which 11 were waited for; matrix products, arithmetic and copies ran while one was open for 29% of the time, Pallas kernels for 0%

profile of v1, /device:TPU:0, one launch (start us, length us, event | category | flops | bytes accessed | tf_op | source)
XLA Modules:
  0.0 231.7 jit_solution(6874495108807070981)
XLA Ops:
  7.2 3.1 %collective-permute-start.10 = (s32[256]{0:T(256)}, s32[256]{0:T(256)S(1)}, u32[]{:S(2)}, u32[]{:S(2)}) collective-permute-start(s32[256]{0:T(256)} %param.13), channel_id=1, source_target_pairs={{0,4},{4,8},{8,12},{12,0},{1,5},{5,9},{9,13},{13,1},{2,6},{6,10},{... | collective-permute-start | bytes 3080 | tf_op jit(solution)/shard_map/ppermute | solution.py:180
  10.3 15.6 %all_gather.6 = bf16[1024,256]{1,0:T(8,128)(2,1)S(1)} all-gather(bf16[256,256]{1,0:T(8,128)(2,1)} %param.20), channel_id=1, replica_groups=mesh['groups'=2,'seq'=4,'head'=2,'rep'=2] {'seq'}, dimensions={0}, use_global_device_ids=true | all-gather | bytes 655360 | tf_op jit(solution)/shard_map/all_gather | solution.py:176
  25.9 15.5 %all_gather.7 = bf16[1024,256]{1,0:T(8,128)(2,1)S(1)} all-gather(bf16[256,256]{1,0:T(8,128)(2,1)} %param.21), channel_id=1, replica_groups=mesh['groups'=2,'seq'=4,'head'=2,'rep'=2] {'seq'}, dimensions={0}, use_global_device_ids=true | all-gather | bytes 655360 | tf_op jit(solution)/shard_map/all_gather | solution.py:177
  49.1 1.8 copy.70
  51.1 2.1 copy.69
  56.6 3.8 %fusion.18 = (f32[4,4,256]{2,1,0:T(4,128)S(1)}, f32[4,4,256]{2,1,0:T(4,128)S(1)}) fusion(f32[4,512,256,4]{2,1,3,0:T(8,128)S(1)} %get-tuple-element.486, f32[4,4,256]{2,1,0:T(4,128)S(1)} %get-tuple-element.463, pred[256,512]{0,1:T(8,128)(4,1)S(1)} %get-tuple-element.478, f32[4,4,256]{2,1,0:T(4,128)S(1)} %max.50, ...), kind=kLoop, calls=%fused_computation.29 | loop fusion | flops 16769024 | bytes 17104896 | tf_op jit(solution)/shard_map/reduce_sum | solution.py:37
  60.5 2.1 fusion.39
  62.7 3.2 %fusion.46 = f32[4,4,256]{2,1,0:T(4,128)S(1)} fusion(bf16[256,4,4,64]{0,3,2,1:T(8,128)(2,1)} %bitcast.39, f32[4,4,256,64]{2,3,1,0:T(8,128)S(1)} %fusion.39, bf16[512,4,64,1]{0,2,3,1:T(8,128)(2,1)S(1)} %bitcast.243, f32[4,512,256,4]{2,1,3,0:T(8,128)S(1)} %get-tuple-element.488, f32[4,4,256]{2,1,0:T(4,128)S(1)} %max.50, ...), kind=kOutput, calls=%fused_computation.58 | convolution fusion | flops 278130688 | bytes 10403840 | tf_op jit(solution)/shard_map/gjqk,kgd->gjqd/dot_general | solution.py:38
  66.0 90.0 %while.26 = (s32[]{:T(128)}, f32[256,4,4,64]{0,3,2,1:T(8,128)S(1)}, bf16[256,256]{0,1:T(8,128)(2,1)S(1)}, bf16[256,256]{0,1:T(8,128)(2,1)S(1)}, s32[256]{0:T(256...) while((s32[]{:T(128)}, f32[256,4,4,64]{0,3,2,1:T(8,128)S(1)}, ...), condition=%wide.region_11.12_spmd.clone, body=%wide.region_10.11_spmd.clone.sunk | while | flops 683147776 | bytes 28963340 | solution.py:233
  66.0 3.7 %collective-permute-start = (bf16[256,256]{0,1:T(8,128)(2,1)S(1)}, bf16[256,256]{0,1:T(8,128)(2,1)S(1)}, u32[]{:S(2)}, u32[]{:S(2)}) collective-permute-start(bf16[256,256]{0,1:T(8,128)(2,1)S(1)} %copy.118), channel_id=1, source_target_pairs={{0,4},{4,8},{8,12},{1,5},{5,9},{9,13},{2,6},{6,10},{10,14},{3,7},{... | collective-permute-start | bytes 393224 | tf_op jit(solution)/shard_map/while/body/eval_jaxpr/ppermute | solution.py:15
  69.8 3.7 %collective-permute-start.1 = (bf16[256,256]{0,1:T(8,128)(2,1)S(1)}, bf16[256,256]{0,1:T(8,128)(2,1)S(1)}, u32[]{:S(2)}, u32[]{:S(2)}) collective-permute-start(bf16[256,256]{0,1:T(8,128)(2,1)S(1)} %copy.119), channel_id=1, source_target_pairs={{0,4},{4,8},{8,12},{1,5},{5,9},{9,13},{2,6},{6,10},{10,14},{3,7},{... | collective-permute-start | bytes 393224 | tf_op jit(solution)/shard_map/while/body/eval_jaxpr/ppermute | solution.py:15
  73.5 3.4 %collective-permute-start.2 = (s32[256]{0:T(256)S(1)}, s32[256]{0:T(256)S(1)}, u32[]{:S(2)}, u32[]{:S(2)}) collective-permute-start(s32[256]{0:T(256)S(1)} %copy.120), channel_id=1, source_target_pairs={{0,4},{4,8},{8,12},{1,5},{5,9},{9,13},{2,6},{6,10},{10,14},{3,7},{... | collective-permute-start | bytes 3080 | tf_op jit(solution)/shard_map/while/body/eval_jaxpr/ppermute | solution.py:15
  77.8 2.4 %fusion.121 = bf16[4,4,256,256]{2,3,1,0:T(8,128)(2,1)S(1)} fusion(f32[4,256,256,4]{2,1,3,0:T(8,128)S(1)} %fusion.120, bf16[256,4,64,1]{0,2,3,1:T(8,128)(2,1)S(1)} %bitcast.231, bf16[256,4,4,64]{0,3,2,1:T(8,128)(2,1)} %get-tuple-element.625, f32[4,4,256]{2,1,0:T(4,128)S(1)} %get-tuple-element.626, f32[4,4,256]{2,1,0:T(4,128)S(1)} %get-tuple-element.624, ...), kind=kOutput, calls=%fused_computation.3.clone.1 | convolution fusion | flops 140509184 | bytes 7045120 | tf_op jit(solution)/shard_map/while/body/eval_jaxpr/qgjd,kgd->gjqk/dot_general | solution.py:48
  81.1 1.9 fusion.125
  83.7 4.2 %collective-permute-done.3 = bf16[256,256]{0,1:T(8,128)(2,1)S(1)} collective-permute-done((bf16[256,256]{0,1:T(8,128)(2,1)S(1)}, bf16[256,256]{0,1:T(8,128)(2,1)S(1)}, u32[]{:S(2)}, u32[]{:S(2)}) %collective-permute-start.3) | collective-permute-done | bytes 131104 | tf_op jit(solution)/shard_map/while/body/eval_jaxpr/ppermute | solution.py:21
  87.8 2.0 collective-permute-done.4
  90.0 2.0 collective-permute-start
  92.0 2.5 %collective-permute-start.1 = (bf16[256,256]{0,1:T(8,128)(2,1)S(1)}, bf16[256,256]{0,1:T(8,128)(2,1)S(1)}, u32[]{:S(2)}, u32[]{:S(2)}) collective-permute-start(bf16[256,256]{0,1:T(8,128)(2,1)S(1)} %copy.119), channel_id=1, source_target_pairs={{0,4},{4,8},{8,12},{1,5},{5,9},{9,13},{2,6},{6,10},{10,14},{3,7},{... | collective-permute-start | bytes 393224 | tf_op jit(solution)/shard_map/while/body/eval_jaxpr/ppermute | solution.py:15
  94.5 4.4 %collective-permute-start.2 = (s32[256]{0:T(256)S(1)}, s32[256]{0:T(256)S(1)}, u32[]{:S(2)}, u32[]{:S(2)}) collective-permute-start(s32[256]{0:T(256)S(1)} %copy.120), channel_id=1, source_target_pairs={{0,4},{4,8},{8,12},{1,5},{5,9},{9,13},{2,6},{6,10},{10,14},{3,7},{... | collective-permute-start | bytes 3080 | tf_op jit(solution)/shard_map/while/body/eval_jaxpr/ppermute | solution.py:15
  99.8 2.4 %fusion.121 = bf16[4,4,256,256]{2,3,1,0:T(8,128)(2,1)S(1)} fusion(f32[4,256,256,4]{2,1,3,0:T(8,128)S(1)} %fusion.120, bf16[256,4,64,1]{0,2,3,1:T(8,128)(2,1)S(1)} %bitcast.231, bf16[256,4,4,64]{0,3,2,1:T(8,128)(2,1)} %get-tuple-element.625, f32[4,4,256]{2,1,0:T(4,128)S(1)} %get-tuple-element.626, f32[4,4,256]{2,1,0:T(4,128)S(1)} %get-tuple-element.624, ...), kind=kOutput, calls=%fused_computation.3.clone.1 | convolution fusion | flops 140509184 | bytes 7045120 | tf_op jit(solution)/shard_map/while/body/eval_jaxpr/qgjd,kgd->gjqk/dot_general | solution.py:48
  103.1 1.9 fusion.125
  105.7 4.2 %collective-permute-done.3 = bf16[256,256]{0,1:T(8,128)(2,1)S(1)} collective-permute-done((bf16[256,256]{0,1:T(8,128)(2,1)S(1)}, bf16[256,256]{0,1:T(8,128)(2,1)S(1)}, u32[]{:S(2)}, u32[]{:S(2)}) %collective-permute-start.3) | collective-permute-done | bytes 131104 | tf_op jit(solution)/shard_map/while/body/eval_jaxpr/ppermute | solution.py:21
  109.9 2.0 collective-permute-done.4
  113.3 3.2 %collective-permute-start.1 = (bf16[256,256]{0,1:T(8,128)(2,1)S(1)}, bf16[256,256]{0,1:T(8,128)(2,1)S(1)}, u32[]{:S(2)}, u32[]{:S(2)}) collective-permute-start(bf16[256,256]{0,1:T(8,128)(2,1)S(1)} %copy.119), channel_id=1, source_target_pairs={{0,4},{4,8},{8,12},{1,5},{5,9},{9,13},{2,6},{6,10},{10,14},{3,7},{... | collective-permute-start | bytes 393224 | tf_op jit(solution)/shard_map/while/body/eval_jaxpr/ppermute | solution.py:15
  116.5 4.3 %collective-permute-start.2 = (s32[256]{0:T(256)S(1)}, s32[256]{0:T(256)S(1)}, u32[]{:S(2)}, u32[]{:S(2)}) collective-permute-start(s32[256]{0:T(256)S(1)} %copy.120), channel_id=1, source_target_pairs={{0,4},{4,8},{8,12},{1,5},{5,9},{9,13},{2,6},{6,10},{10,14},{3,7},{... | collective-permute-start | bytes 3080 | tf_op jit(solution)/shard_map/while/body/eval_jaxpr/ppermute | solution.py:15
  121.8 2.4 %fusion.121 = bf16[4,4,256,256]{2,3,1,0:T(8,128)(2,1)S(1)} fusion(f32[4,256,256,4]{2,1,3,0:T(8,128)S(1)} %fusion.120, bf16[256,4,64,1]{0,2,3,1:T(8,128)(2,1)S(1)} %bitcast.231, bf16[256,4,4,64]{0,3,2,1:T(8,128)(2,1)} %get-tuple-element.625, f32[4,4,256]{2,1,0:T(4,128)S(1)} %get-tuple-element.626, f32[4,4,256]{2,1,0:T(4,128)S(1)} %get-tuple-element.624, ...), kind=kOutput, calls=%fused_computation.3.clone.1 | convolution fusion | flops 140509184 | bytes 7045120 | tf_op jit(solution)/shard_map/while/body/eval_jaxpr/qgjd,kgd->gjqk/dot_general | solution.py:48
  125.1 1.9 fusion.125
  127.7 4.2 %collective-permute-done.3 = bf16[256,256]{0,1:T(8,128)(2,1)S(1)} collective-permute-done((bf16[256,256]{0,1:T(8,128)(2,1)S(1)}, bf16[256,256]{0,1:T(8,128)(2,1)S(1)}, u32[]{:S(2)}, u32[]{:S(2)}) %collective-permute-start.3) | collective-permute-done | bytes 131104 | tf_op jit(solution)/shard_map/while/body/eval_jaxpr/ppermute | solution.py:21
  131.9 2.0 collective-permute-done.4
  135.3 3.2 %collective-permute-start.1 = (bf16[256,256]{0,1:T(8,128)(2,1)S(1)}, bf16[256,256]{0,1:T(8,128)(2,1)S(1)}, u32[]{:S(2)}, u32[]{:S(2)}) collective-permute-start(bf16[256,256]{0,1:T(8,128)(2,1)S(1)} %copy.119), channel_id=1, source_target_pairs={{0,4},{4,8},{8,12},{1,5},{5,9},{9,13},{2,6},{6,10},{10,14},{3,7},{... | collective-permute-start | bytes 393224 | tf_op jit(solution)/shard_map/while/body/eval_jaxpr/ppermute | solution.py:15
  138.5 4.3 %collective-permute-start.2 = (s32[256]{0:T(256)S(1)}, s32[256]{0:T(256)S(1)}, u32[]{:S(2)}, u32[]{:S(2)}) collective-permute-start(s32[256]{0:T(256)S(1)} %copy.120), channel_id=1, source_target_pairs={{0,4},{4,8},{8,12},{1,5},{5,9},{9,13},{2,6},{6,10},{10,14},{3,7},{... | collective-permute-start | bytes 3080 | tf_op jit(solution)/shard_map/while/body/eval_jaxpr/ppermute | solution.py:15
  143.8 2.4 %fusion.121 = bf16[4,4,256,256]{2,3,1,0:T(8,128)(2,1)S(1)} fusion(f32[4,256,256,4]{2,1,3,0:T(8,128)S(1)} %fusion.120, bf16[256,4,64,1]{0,2,3,1:T(8,128)(2,1)S(1)} %bitcast.231, bf16[256,4,4,64]{0,3,2,1:T(8,128)(2,1)} %get-tuple-element.625, f32[4,4,256]{2,1,0:T(4,128)S(1)} %get-tuple-element.626, f32[4,4,256]{2,1,0:T(4,128)S(1)} %get-tuple-element.624, ...), kind=kOutput, calls=%fused_computation.3.clone.1 | convolution fusion | flops 140509184 | bytes 7045120 | tf_op jit(solution)/shard_map/while/body/eval_jaxpr/qgjd,kgd->gjqk/dot_general | solution.py:48
  147.1 1.9 fusion.125
  149.7 4.2 %collective-permute-done.3 = bf16[256,256]{0,1:T(8,128)(2,1)S(1)} collective-permute-done((bf16[256,256]{0,1:T(8,128)(2,1)S(1)}, bf16[256,256]{0,1:T(8,128)(2,1)S(1)}, u32[]{:S(2)}, u32[]{:S(2)}) %collective-permute-start.3) | collective-permute-done | bytes 131104 | tf_op jit(solution)/shard_map/while/body/eval_jaxpr/ppermute | solution.py:21
  153.9 2.0 collective-permute-done.4
  157.3 3.2 %collective-permute-start.5 = (bf16[128,256]{1,0:T(8,128)(2,1)S(1)}, bf16[128,256]{1,0:T(8,128)(2,1)S(1)}, u32[]{:S(2)}, u32[]{:S(2)}) collective-permute-start(bf16[128,256]{1,0:T(8,128)(2,1)S(1)} %slice.71), channel_id=1, source_target_pairs={{0,4},{4,8},{8,12},{1,5},{5,9},{9,13},{2,6},{6,10},{10,14},{3,7},{... | collective-permute-start | bytes 196616 | tf_op jit(solution)/shard_map/ppermute | solution.py:15
  161.2 5.0 %collective-permute-start.7 = (bf16[128,256]{1,0:T(8,128)(2,1)}, bf16[128,256]{1,0:T(8,128)(2,1)}, u32[]{:S(2)}, u32[]{:S(2)}) collective-permute-start(bf16[128,256]{1,0:T(8,128)(2,1)} %slice.73), channel_id=1, source_target_pairs={{0,4},{4,8},{8,12},{1,5},{5,9},{9,13},{2,6},{6,10},{10,14},{3,7},{... | collective-permute-start | bytes 196616 | tf_op jit(solution)/shard_map/ppermute | solution.py:15
  173.6 2.5 %fusion.66 = (bf16[384,4,64]{0,2,1:T(8,128)(2,1)S(1)}, f32[384,4,64]{0,2,1:T(8,128)}) fusion(bf16[256,4,4,64]{0,3,2,1:T(8,128)(2,1)S(1)} %bitcast.238, f32[4,384,256,4]{2,1,3,0:T(8,128)S(1)} %get-tuple-element.480, f32[4,4,256]{2,1,0:T(4,128)S(1)} %log_add_fusion.1, pred[256,384]{0,1:T(8,128)(4,1)S(1)} %fusion.52), kind=kOutput, calls=%fused_computation.104 | convolution fusion | flops 209289216 | bytes 7520256 | tf_op jit(solution)/shard_map/gjqk,qgjd->kgd/dot_general | solution.py:54
  179.7 1.9 copy.54
  181.7 4.8 %fusion.43 = f32[4,4,256]{2,1,0:T(4,128)S(1)} fusion(bf16[384,4,64,1]{0,2,3,1:T(8,128)(2,1)} %bitcast.249, bf16[256,4,4,64]{0,3,2,1:T(8,128)(2,1)} %bitcast.239, f32[4,384,256,4]{2,1,3,0:T(8,128)} %copy-done, f32[4,4,256]{2,1,0:T(4,128)S(1)} %log_add_fusion.1, pred[256,384]{0,1:T(8,128)(4,1)S(1)} %fusion.52), kind=kOutput, calls=%fused_computation.52 | convolution fusion | flops 209973248 | bytes 7143424 | tf_op jit(solution)/shard_map/gjqk,kgd->gjqd/dot_general | solution.py:110
  186.5 2.0 fusion.24
  188.5 1.6 copy-done.1
  195.6 3.7 %collective-permute-done.8 = bf16[128,256]{1,0:T(8,128)(2,1)S(1)} collective-permute-done((bf16[128,256]{1,0:T(8,128)(2,1)S(1)}, bf16[128,256]{1,0:T(8,128)(2,1)S(1)}, u32[]{:S(2)}, u32[]{:S(2)}) %collective-permute-start.8) | collective-permute-done | bytes 65568 | tf_op jit(solution)/shard_map/ppermute | solution.py:15
  201.1 2.6 %fusion.42 = bf16[4,64,4,256]{3,1,2,0:T(8,128)(2,1)S(1)} fusion(bf16[384,4,64,1]{0,2,3,1:T(8,128)(2,1)S(1)} %bitcast.234, bf16[4,4,256,384]{2,3,1,0:T(8,128)(2,1)} %copy-done.1), kind=kOutput, calls=%fused_computation.51 | convolution fusion | flops 201850880 | bytes 3866624 | tf_op jit(solution)/shard_map/gjqk,kgd->qgjd/dot_general | solution.py:62
  204.8 13.8 %all-reduce.3.cloned.1.call-done = (bf16[256,256]{1,0:T(8,128)(2,1)}, bf16[256,256]{1,0:T(8,128)(2,1)}, bf16[256,256]{1,0:T(8,128)(2,1)}, bf16[256,256]{1,0:T(8,128)(2,1)}) async-done(((bf16[256,256]{1,0:T(8,128)(2,1)}, bf16[256,256]{1,0:T(8,128)(2,1)}, bf16[256,256]{1,0:T(8,128)(2,1)}, bf16[256,256]{1,0:T(8,128)(2,1)}), (bf16[256,256]{1,0:T(8,128)(2,1)}, bf16[256,256]{1,0:T(8,128)(2,1)}, ...) | async-done | bytes 524304 | tf_op jit(solution)/shard_map/psum | solution.py:237
  218.6 1.6 copy.134
  220.1 1.6 copy.135
  221.7 1.6 copy.136
  (190 shorter events, 46.4 us)
Async XLA Ops:
  7.2 46.1 %copy-start.11 = (s32[256]{0:T(256)S(1)}, s32[256]{0:T(256)}, u32[]{:S(2)}) copy-start(s32[256]{0:T(256)} %param.13) | copy-start | bytes 3076
  7.2 211.4 %all-reduce.3.cloned.1.call-start = ((), (), s32[]{:S(2)}) async-start(), calls=%async_computation | async-start | bytes 1048576 | tf_op jit(solution)/shard_map/psum | solution.py:237
  7.2 34.9 %collective-permute-start.10 = (s32[256]{0:T(256)}, s32[256]{0:T(256)S(1)}, u32[]{:S(2)}, u32[]{:S(2)}) collective-permute-start(s32[256]{0:T(256)} %param.13), channel_id=1, source_target_pairs={{0,4},{4,8},{8,12},{12,0},{1,5},{5,9},{9,13},{13,1},{2,6},{6,10},{... | collective-permute-start | bytes 3080 | tf_op jit(solution)/shard_map/ppermute | solution.py:180
  42.1 5.4 %collective-permute-start.11 = (s32[256]{0:T(256)S(1)}, s32[256]{0:T(256)S(1)}, u32[]{:S(2)}, u32[]{:S(2)}) collective-permute-start(s32[256]{0:T(256)S(1)} %collective-permute-done.10), channel_id=1, source_target_pairs={{0,4},{4,8},{8,12},{12,0},{1,5},{5,9},{9,13},{13,1},{2,6},{6,10},{... | collective-permute-start | bytes 3080 | tf_op jit(solution)/shard_map/ppermute | solution.py:180
  47.5 5.7 %collective-permute-start.12 = (s32[256]{0:T(256)S(1)}, s32[256]{0:T(256)S(1)}, u32[]{:S(2)}, u32[]{:S(2)}) collective-permute-start(s32[256]{0:T(256)S(1)} %collective-permute-done.11), channel_id=1, source_target_pairs={{0,4},{4,8},{8,12},{12,0},{1,5},{5,9},{9,13},{13,1},{2,6},{6,10},{... | collective-permute-start | bytes 3080 | tf_op jit(solution)/shard_map/ppermute | solution.py:180
  53.7 1.4 copy-start.12
  56.6 4.0 %copy-start.9 = (bf16[512,256]{0,1:T(8,128)(2,1)S(1)}, bf16[512,256]{0,1:T(8,128)(2,1)}, u32[]{:S(2)}) copy-start(bf16[512,256]{0,1:T(8,128)(2,1)} %copy.70) | copy-start | bytes 786436
  65.9 90.0 %copy-start.14 = (s32[128]{0:T(128)S(1)}, s32[128]{0:T(128)}, u32[]{:S(2)}) copy-start(s32[128]{0:T(128)} %slice.72) | copy-start | bytes 1540
  65.9 91.3 %copy-start.6 = (bf16[256,256]{1,0:T(8,128)(2,1)S(1)}, bf16[256,256]{1,0:T(8,128)(2,1)}, u32[]{:S(2)}) copy-start(bf16[256,256]{1,0:T(8,128)(2,1)} %param.15) | copy-start | bytes 393220
  65.9 94.6 %copy-start.7 = (bf16[256,256]{1,0:T(8,128)(2,1)S(1)}, bf16[256,256]{1,0:T(8,128)(2,1)}, u32[]{:S(2)}) copy-start(bf16[256,256]{1,0:T(8,128)(2,1)} %param.16) | copy-start | bytes 393220
  66.0 23.9 %collective-permute-start = (bf16[256,256]{0,1:T(8,128)(2,1)S(1)}, bf16[256,256]{0,1:T(8,128)(2,1)S(1)}, u32[]{:S(2)}, u32[]{:S(2)}) collective-permute-start(bf16[256,256]{0,1:T(8,128)(2,1)S(1)} %copy.118), channel_id=1, source_target_pairs={{0,4},{4,8},{8,12},{1,5},{5,9},{9,13},{2,6},{6,10},{10,14},{3,7},{... | collective-permute-start | bytes 393224 | tf_op jit(solution)/shard_map/while/body/eval_jaxpr/ppermute | solution.py:15
  69.8 20.2 %collective-permute-start.1 = (bf16[256,256]{0,1:T(8,128)(2,1)S(1)}, bf16[256,256]{0,1:T(8,128)(2,1)S(1)}, u32[]{:S(2)}, u32[]{:S(2)}) collective-permute-start(bf16[256,256]{0,1:T(8,128)(2,1)S(1)} %copy.119), channel_id=1, source_target_pairs={{0,4},{4,8},{8,12},{1,5},{5,9},{9,13},{2,6},{6,10},{10,14},{3,7},{... | collective-permute-start | bytes 393224 | tf_op jit(solution)/shard_map/while/body/eval_jaxpr/ppermute | solution.py:15
  73.5 16.4 %collective-permute-start.2 = (s32[256]{0:T(256)S(1)}, s32[256]{0:T(256)S(1)}, u32[]{:S(2)}, u32[]{:S(2)}) collective-permute-start(s32[256]{0:T(256)S(1)} %copy.120), channel_id=1, source_target_pairs={{0,4},{4,8},{8,12},{1,5},{5,9},{9,13},{2,6},{6,10},{10,14},{3,7},{... | collective-permute-start | bytes 3080 | tf_op jit(solution)/shard_map/while/body/eval_jaxpr/ppermute | solution.py:15
  81.0 6.8 %collective-permute-start.3 = (bf16[256,256]{0,1:T(8,128)(2,1)S(1)}, bf16[256,256]{0,1:T(8,128)(2,1)S(1)}, u32[]{:S(2)}, u32[]{:S(2)}) collective-permute-start(bf16[256,256]{0,1:T(8,128)(2,1)S(1)} %fusion.124), channel_id=1, source_target_pairs={{12,0},{0,4},{4,8},{8,12},{13,1},{1,5},{5,9},{9,13},{14,2},{2,6},{... | collective-permute-start | bytes 393224 | tf_op jit(solution)/shard_map/while/body/eval_jaxpr/ppermute | solution.py:21
  83.0 6.8 %collective-permute-start.4 = (bf16[256,256]{0,1:T(8,128)(2,1)S(1)}, bf16[256,256]{0,1:T(8,128)(2,1)S(1)}, u32[]{:S(2)}, u32[]{:S(2)}) collective-permute-start(bf16[256,256]{0,1:T(8,128)(2,1)S(1)} %fusion.126), channel_id=1, source_target_pairs={{12,0},{0,4},{4,8},{8,12},{13,1},{1,5},{5,9},{9,13},{14,2},{2,6},{... | collective-permute-start | bytes 393224 | tf_op jit(solution)/shard_map/while/body/eval_jaxpr/ppermute | solution.py:21
  90.0 22.0 %collective-permute-start = (bf16[256,256]{0,1:T(8,128)(2,1)S(1)}, bf16[256,256]{0,1:T(8,128)(2,1)S(1)}, u32[]{:S(2)}, u32[]{:S(2)}) collective-permute-start(bf16[256,256]{0,1:T(8,128)(2,1)S(1)} %copy.118), channel_id=1, source_target_pairs={{0,4},{4,8},{8,12},{1,5},{5,9},{9,13},{2,6},{6,10},{10,14},{3,7},{... | collective-permute-start | bytes 393224 | tf_op jit(solution)/shard_map/while/body/eval_jaxpr/ppermute | solution.py:15
  92.0 20.0 %collective-permute-start.1 = (bf16[256,256]{0,1:T(8,128)(2,1)S(1)}, bf16[256,256]{0,1:T(8,128)(2,1)S(1)}, u32[]{:S(2)}, u32[]{:S(2)}) collective-permute-start(bf16[256,256]{0,1:T(8,128)(2,1)S(1)} %copy.119), channel_id=1, source_target_pairs={{0,4},{4,8},{8,12},{1,5},{5,9},{9,13},{2,6},{6,10},{10,14},{3,7},{... | collective-permute-start | bytes 393224 | tf_op jit(solution)/shard_map/while/body/eval_jaxpr/ppermute | solution.py:15
  94.5 17.4 %collective-permute-start.2 = (s32[256]{0:T(256)S(1)}, s32[256]{0:T(256)S(1)}, u32[]{:S(2)}, u32[]{:S(2)}) collective-permute-start(s32[256]{0:T(256)S(1)} %copy.120), channel_id=1, source_target_pairs={{0,4},{4,8},{8,12},{1,5},{5,9},{9,13},{2,6},{6,10},{10,14},{3,7},{... | collective-permute-start | bytes 3080 | tf_op jit(solution)/shard_map/while/body/eval_jaxpr/ppermute | solution.py:15
  103.0 6.8 %collective-permute-start.3 = (bf16[256,256]{0,1:T(8,128)(2,1)S(1)}, bf16[256,256]{0,1:T(8,128)(2,1)S(1)}, u32[]{:S(2)}, u32[]{:S(2)}) collective-permute-start(bf16[256,256]{0,1:T(8,128)(2,1)S(1)} %fusion.124), channel_id=1, source_target_pairs={{12,0},{0,4},{4,8},{8,12},{13,1},{1,5},{5,9},{9,13},{14,2},{2,6},{... | collective-permute-start | bytes 393224 | tf_op jit(solution)/shard_map/while/body/eval_jaxpr/ppermute | solution.py:21
  105.1 6.8 %collective-permute-start.4 = (bf16[256,256]{0,1:T(8,128)(2,1)S(1)}, bf16[256,256]{0,1:T(8,128)(2,1)S(1)}, u32[]{:S(2)}, u32[]{:S(2)}) collective-permute-start(bf16[256,256]{0,1:T(8,128)(2,1)S(1)} %fusion.126), channel_id=1, source_target_pairs={{12,0},{0,4},{4,8},{8,12},{13,1},{1,5},{5,9},{9,13},{14,2},{2,6},{... | collective-permute-start | bytes 393224 | tf_op jit(solution)/shard_map/while/body/eval_jaxpr/ppermute | solution.py:21
  112.0 22.0 %collective-permute-start = (bf16[256,256]{0,1:T(8,128)(2,1)S(1)}, bf16[256,256]{0,1:T(8,128)(2,1)S(1)}, u32[]{:S(2)}, u32[]{:S(2)}) collective-permute-start(bf16[256,256]{0,1:T(8,128)(2,1)S(1)} %copy.118), channel_id=1, source_target_pairs={{0,4},{4,8},{8,12},{1,5},{5,9},{9,13},{2,6},{6,10},{10,14},{3,7},{... | collective-permute-start | bytes 393224 | tf_op jit(solution)/shard_map/while/body/eval_jaxpr/ppermute | solution.py:15
  113.3 20.6 %collective-permute-start.1 = (bf16[256,256]{0,1:T(8,128)(2,1)S(1)}, bf16[256,256]{0,1:T(8,128)(2,1)S(1)}, u32[]{:S(2)}, u32[]{:S(2)}) collective-permute-start(bf16[256,256]{0,1:T(8,128)(2,1)S(1)} %copy.119), channel_id=1, source_target_pairs={{0,4},{4,8},{8,12},{1,5},{5,9},{9,13},{2,6},{6,10},{10,14},{3,7},{... | collective-permute-start | bytes 393224 | tf_op jit(solution)/shard_map/while/body/eval_jaxpr/ppermute | solution.py:15
  116.5 17.4 %collective-permute-start.2 = (s32[256]{0:T(256)S(1)}, s32[256]{0:T(256)S(1)}, u32[]{:S(2)}, u32[]{:S(2)}) collective-permute-start(s32[256]{0:T(256)S(1)} %copy.120), channel_id=1, source_target_pairs={{0,4},{4,8},{8,12},{1,5},{5,9},{9,13},{2,6},{6,10},{10,14},{3,7},{... | collective-permute-start | bytes 3080 | tf_op jit(solution)/shard_map/while/body/eval_jaxpr/ppermute | solution.py:15
  125.0 6.8 %collective-permute-start.3 = (bf16[256,256]{0,1:T(8,128)(2,1)S(1)}, bf16[256,256]{0,1:T(8,128)(2,1)S(1)}, u32[]{:S(2)}, u32[]{:S(2)}) collective-permute-start(bf16[256,256]{0,1:T(8,128)(2,1)S(1)} %fusion.124), channel_id=1, source_target_pairs={{12,0},{0,4},{4,8},{8,12},{13,1},{1,5},{5,9},{9,13},{14,2},{2,6},{... | collective-permute-start | bytes 393224 | tf_op jit(solution)/shard_map/while/body/eval_jaxpr/ppermute | solution.py:21
  127.1 6.8 %collective-permute-start.4 = (bf16[256,256]{0,1:T(8,128)(2,1)S(1)}, bf16[256,256]{0,1:T(8,128)(2,1)S(1)}, u32[]{:S(2)}, u32[]{:S(2)}) collective-permute-start(bf16[256,256]{0,1:T(8,128)(2,1)S(1)} %fusion.126), channel_id=1, source_target_pairs={{12,0},{0,4},{4,8},{8,12},{13,1},{1,5},{5,9},{9,13},{14,2},{2,6},{... | collective-permute-start | bytes 393224 | tf_op jit(solution)/shard_map/while/body/eval_jaxpr/ppermute | solution.py:21
  134.0 22.0 %collective-permute-start = (bf16[256,256]{0,1:T(8,128)(2,1)S(1)}, bf16[256,256]{0,1:T(8,128)(2,1)S(1)}, u32[]{:S(2)}, u32[]{:S(2)}) collective-permute-start(bf16[256,256]{0,1:T(8,128)(2,1)S(1)} %copy.118), channel_id=1, source_target_pairs={{0,4},{4,8},{8,12},{1,5},{5,9},{9,13},{2,6},{6,10},{10,14},{3,7},{... | collective-permute-start | bytes 393224 | tf_op jit(solution)/shard_map/while/body/eval_jaxpr/ppermute | solution.py:15
  135.3 20.6 %collective-permute-start.1 = (bf16[256,256]{0,1:T(8,128)(2,1)S(1)}, bf16[256,256]{0,1:T(8,128)(2,1)S(1)}, u32[]{:S(2)}, u32[]{:S(2)}) collective-permute-start(bf16[256,256]{0,1:T(8,128)(2,1)S(1)} %copy.119), channel_id=1, source_target_pairs={{0,4},{4,8},{8,12},{1,5},{5,9},{9,13},{2,6},{6,10},{10,14},{3,7},{... | collective-permute-start | bytes 393224 | tf_op jit(solution)/shard_map/while/body/eval_jaxpr/ppermute | solution.py:15
  138.5 17.4 %collective-permute-start.2 = (s32[256]{0:T(256)S(1)}, s32[256]{0:T(256)S(1)}, u32[]{:S(2)}, u32[]{:S(2)}) collective-permute-start(s32[256]{0:T(256)S(1)} %copy.120), channel_id=1, source_target_pairs={{0,4},{4,8},{8,12},{1,5},{5,9},{9,13},{2,6},{6,10},{10,14},{3,7},{... | collective-permute-start | bytes 3080 | tf_op jit(solution)/shard_map/while/body/eval_jaxpr/ppermute | solution.py:15
  147.0 6.8 %collective-permute-start.3 = (bf16[256,256]{0,1:T(8,128)(2,1)S(1)}, bf16[256,256]{0,1:T(8,128)(2,1)S(1)}, u32[]{:S(2)}, u32[]{:S(2)}) collective-permute-start(bf16[256,256]{0,1:T(8,128)(2,1)S(1)} %fusion.124), channel_id=1, source_target_pairs={{12,0},{0,4},{4,8},{8,12},{13,1},{1,5},{5,9},{9,13},{14,2},{2,6},{... | collective-permute-start | bytes 393224 | tf_op jit(solution)/shard_map/while/body/eval_jaxpr/ppermute | solution.py:21
  149.1 6.8 %collective-permute-start.4 = (bf16[256,256]{0,1:T(8,128)(2,1)S(1)}, bf16[256,256]{0,1:T(8,128)(2,1)S(1)}, u32[]{:S(2)}, u32[]{:S(2)}) collective-permute-start(bf16[256,256]{0,1:T(8,128)(2,1)S(1)} %fusion.126), channel_id=1, source_target_pairs={{12,0},{0,4},{4,8},{8,12},{13,1},{1,5},{5,9},{9,13},{14,2},{2,6},{... | collective-permute-start | bytes 393224 | tf_op jit(solution)/shard_map/while/body/eval_jaxpr/ppermute | solution.py:21
  156.0 16.1 %copy-start.13 = (f32[4,4]{1,0:T(4,128)S(1)}, f32[4,4]{1,0:T(4,128)}, u32[]{:S(2)}) copy-start(f32[4,4]{1,0:T(4,128)} %param.18) | copy-start | bytes 196
  156.0 13.0 %collective-permute-start.6 = (s32[128]{0:T(128)S(1)}, s32[128]{0:T(128)S(1)}, u32[]{:S(2)}, u32[]{:S(2)}) collective-permute-start(s32[128]{0:T(128)S(1)} %copy-done.14), channel_id=1, source_target_pairs={{0,4},{4,8},{8,12},{1,5},{5,9},{9,13},{2,6},{6,10},{10,14},{3,7},{... | collective-permute-start | bytes 1544 | tf_op jit(solution)/shard_map/ppermute | solution.py:15
  157.3 13.5 %collective-permute-start.5 = (bf16[128,256]{1,0:T(8,128)(2,1)S(1)}, bf16[128,256]{1,0:T(8,128)(2,1)S(1)}, u32[]{:S(2)}, u32[]{:S(2)}) collective-permute-start(bf16[128,256]{1,0:T(8,128)(2,1)S(1)} %slice.71), channel_id=1, source_target_pairs={{0,4},{4,8},{8,12},{1,5},{5,9},{9,13},{2,6},{6,10},{10,14},{3,7},{... | collective-permute-start | bytes 196616 | tf_op jit(solution)/shard_map/ppermute | solution.py:15
  161.2 17.0 %collective-permute-start.7 = (bf16[128,256]{1,0:T(8,128)(2,1)}, bf16[128,256]{1,0:T(8,128)(2,1)}, u32[]{:S(2)}, u32[]{:S(2)}) collective-permute-start(bf16[128,256]{1,0:T(8,128)(2,1)} %slice.73), channel_id=1, source_target_pairs={{0,4},{4,8},{8,12},{1,5},{5,9},{9,13},{2,6},{6,10},{10,14},{3,7},{... | collective-permute-start | bytes 196616 | tf_op jit(solution)/shard_map/ppermute | solution.py:15
  167.5 6.0 %copy-start.2 = (bf16[256,4,256]{0,2,1:T(8,128)(2,1)}, bf16[256,4,256]{0,2,1:T(8,128)(2,1)S(1)}, u32[]{:S(2)}) copy-start(bf16[256,4,256]{0,2,1:T(8,128)(2,1)S(1)} %copy.53) | copy-start | bytes 1572868
  169.0 4.6 %copy-start.4 = (bf16[256,4,256]{0,2,1:T(8,128)(2,1)}, bf16[256,4,256]{0,2,1:T(8,128)(2,1)S(1)}, u32[]{:S(2)}) copy-start(bf16[256,4,256]{0,2,1:T(8,128)(2,1)S(1)} %copy.55) | copy-start | bytes 1572868
  172.1 4.1 %copy-start = (f32[4,384,256,4]{2,1,3,0:T(8,128)}, f32[4,384,256,4]{2,1,3,0:T(8,128)S(1)}, u32[]{:S(2)}) copy-start(f32[4,384,256,4]{2,1,3,0:T(8,128)S(1)} %get-tuple-element.480) | copy-start | bytes 18874372
  173.6 4.6 %copy-start.8 = (bf16[256,256]{1,0:T(8,128)(2,1)S(1)}, bf16[256,256]{1,0:T(8,128)(2,1)}, u32[]{:S(2)}) copy-start(bf16[256,256]{1,0:T(8,128)(2,1)} %param.16) | copy-start | bytes 393220
  176.9 17.2 %collective-permute-start.9 = (bf16[128,256]{1,0:T(8,128)(2,1)}, bf16[128,256]{1,0:T(8,128)(2,1)}, u32[]{:S(2)}, u32[]{:S(2)}) collective-permute-start(bf16[128,256]{1,0:T(8,128)(2,1)} %copy.63), channel_id=1, source_target_pairs={{4,0},{8,4},{12,8},{5,1},{9,5},{13,9},{6,2},{10,6},{14,10},{7,3},{... | collective-permute-start | bytes 196616 | tf_op jit(solution)/shard_map/ppermute | solution.py:15
  179.7 6.7 %slice-start = ((s8[6291456]{0:T(1024)(128)(4,1)}), s8[2097152]{0:T(1024)(128)(4,1)S(1)}, s32[]{:S(2)}) async-start(s8[6291456]{0:T(1024)(128)(4,1)} %bitcast.227), calls=%async_computation.1 | async-start | bytes 4194304
  181.6 4.8 %copy-start.5 = (bf16[256,4,256]{0,2,1:T(8,128)(2,1)S(1)}, bf16[256,4,256]{0,2,1:T(8,128)(2,1)}, u32[]{:S(2)}) copy-start(bf16[256,4,256]{0,2,1:T(8,128)(2,1)} %copy-done.4) | copy-start | bytes 1572868
  181.6 4.8 %copy-start.10 = (bf16[384,256]{0,1:T(8,128)(2,1)S(1)}, bf16[384,256]{0,1:T(8,128)(2,1)}, u32[]{:S(2)}) copy-start(bf16[384,256]{0,1:T(8,128)(2,1)} %copy.54) | copy-start | bytes 589828
  181.6 4.8 %slice-start.1 = ((s8[6291456]{0:T(1024)(128)(4,1)}), s8[4194304]{0:T(1024)(128)(4,1)S(1)}, s32[]{:S(2)}) async-start(s8[6291456]{0:T(1024)(128)(4,1)} %bitcast.227), calls=%async_computation.2 | async-start | bytes 8388608
  186.5 3.7 %copy-start.3 = (bf16[256,4,256]{0,2,1:T(8,128)(2,1)S(1)}, bf16[256,4,256]{0,2,1:T(8,128)(2,1)}, u32[]{:S(2)}) copy-start(bf16[256,4,256]{0,2,1:T(8,128)(2,1)} %copy-done.2) | copy-start | bytes 1572868
  188.5 1.6 copy-start.1
  192.5 6.8 %collective-permute-start.8 = (bf16[128,256]{1,0:T(8,128)(2,1)S(1)}, bf16[128,256]{1,0:T(8,128)(2,1)S(1)}, u32[]{:S(2)}, u32[]{:S(2)}) collective-permute-start(bf16[128,256]{1,0:T(8,128)(2,1)S(1)} %copy.59), channel_id=1, source_target_pairs={{4,0},{8,4},{12,8},{5,1},{9,5},{13,9},{6,2},{10,6},{14,10},{7,3},{... | collective-permute-start | bytes 196616 | tf_op jit(solution)/shard_map/ppermute | solution.py:15
Sparse Core Ops, SparseCore 0:
  200.1 18.3 all-reduce.2
